TPU v7x, 512 devices: a whole 4x4x16 slice. The times are simulated.
512 devices in a mesh: dp: 32 (over x, y, core), expert: 16 (over z).
Axes of the slice: x: 4, y: 4, z: 16, core: 2. Of those that a mesh axis runs over, the one named last changes fastest.
Arguments:
- out_grad: bfloat16 [65536, 2048], P(('dp', 'expert')), may hold values from -6 to 6
- expert_ids: int32 [65536, 4], P(('dp', 'expert')), may hold values from 0 to 15, all different within a row; in each aligned block of 128 rows (0 to 127, 128 to 255, ...) at most 64 rows name the same one
- route_weights: bfloat16 [65536, 4], P(('dp', 'expert')), may hold values from 0.049804688 to 1
- pre_activations: bfloat16 [65536, 4, 1536], P(('dp', 'expert')), may hold values from -6 to 6
- down_weight: bfloat16 [16, 768, 2048], P('expert', 'dp'), may hold values from -0.21875 to 0.21875
Outputs:
- pre_grad: bfloat16 [65536, 4, 1536], P(('dp', 'expert'))
- weight_grad: bfloat16 [65536, 4], P(('dp', 'expert'))
- down_grad: bfloat16 [16, 768, 2048], P('expert', 'dp')
Inputs may be any that keep to these rules, and one draw needn't show every extreme that they name: `expert_ids`: among the 128 rows of one device, each expert is named by at most 64 rows, a bound that some block reaches; the numbers in a row are distinct.
All inputs are finite; a program needn't handle non-finite values.
Results may differ from a plain program's by a relative error of at most 0.015.
Values may be sent and summed in bfloat16 or wider, within the bound.
No kernel may reach another device: no remote copies, remote signals or barrier semaphores. Data moves between devices by JAX's collectives and lax.ppermute only.
A program may use at most 64 MiB of HBM per device.

v0:
```python
import jax
import jax.numpy as jnp
from jax import lax
from jax.sharding import PartitionSpec as P

EXPERTS = 16
CAP = 64


def swiglu_value(pre, units):
    gate_val = pre[..., :units].astype(jnp.float32)
    up_val = pre[..., units:].astype(jnp.float32)
    return gate_val * jax.nn.sigmoid(gate_val) * up_val


def swiglu_back(pre, weights, hidden_grad, units):
    gate_val = pre[..., :units].astype(jnp.float32)
    up_val = pre[..., units:].astype(jnp.float32)
    sigmoid_val = jax.nn.sigmoid(gate_val)
    cotangent = weights.astype(jnp.float32)[..., None] * hidden_grad.astype(jnp.float32)
    gate_grad = cotangent * up_val * sigmoid_val * (1.0 + gate_val * (1.0 - sigmoid_val))
    up_grad = cotangent * gate_val * sigmoid_val
    return jnp.concatenate([gate_grad, up_grad], axis=-1).astype(jnp.bfloat16)


def slot_places(chosen, experts, capacity):
    flat = chosen.reshape(-1)
    onehot = (flat[:, None] == jnp.arange(experts, dtype=jnp.int32)[None, :]).astype(jnp.int32)
    ranks = jnp.cumsum(onehot, axis=0) - 1
    rank = jnp.sum(ranks * onehot, axis=1)
    target = flat * capacity + rank
    count = flat.shape[0]
    source = (
        jnp.full((experts * capacity,), count, jnp.int32)
        .at[target]
        .set(jnp.arange(count, dtype=jnp.int32))
    )
    return (target, source)


def arrange(values, sources):
    local = values.shape[0] // sources
    values = values.reshape((sources, local) + values.shape[1:])
    values = jnp.swapaxes(values, 0, 1)
    return values.reshape((local, sources * values.shape[2]) + values.shape[3:])


def restore(values, sources):
    local = values.shape[0]
    per_source = values.shape[1] // sources
    values = values.reshape((local, sources, per_source) + values.shape[2:])
    values = jnp.swapaxes(values, 0, 1)
    return values.reshape((sources * local, per_source) + values.shape[3:])


def body(out_grad, expert_ids, route_weights, pre_activations, down_weight):
    tok_rows, width = out_grad.shape
    top = expert_ids.shape[1]
    units = pre_activations.shape[2] // 2
    slots = tok_rows * top
    sources = lax.axis_size("expert")
    replicas = lax.axis_size("dp")
    target, source = slot_places(expert_ids, EXPERTS, CAP)
    pad_grad = jnp.concatenate([out_grad, jnp.zeros((1, width), out_grad.dtype)], axis=0)
    send_grad = pad_grad[source // top].reshape(EXPERTS, CAP, width)
    flat_weights = jnp.concatenate(
        [route_weights.reshape(slots), jnp.zeros((1,), route_weights.dtype)], axis=0
    )
    send_weights = flat_weights[source].reshape(EXPERTS, CAP)
    flat_pre = jnp.concatenate(
        [
            pre_activations.reshape(slots, 2 * units),
            jnp.zeros((1, 2 * units), pre_activations.dtype),
        ],
        axis=0,
    )
    send_pre = flat_pre[source].reshape(EXPERTS, CAP, 2 * units)
    got_grad, got_pre, got_weights = (
        lax.all_to_all(send_grad, "expert", split_axis=0, concat_axis=0, tiled=True),
        lax.all_to_all(send_pre, "expert", split_axis=0, concat_axis=0, tiled=True),
        lax.all_to_all(send_weights, "expert", split_axis=0, concat_axis=0, tiled=True),
    )
    local_pre = arrange(got_pre, sources)
    hidden = swiglu_value(local_pre, units).astype(jnp.bfloat16)
    local_grad = arrange(got_grad, sources)
    local_weights = arrange(got_weights, sources)
    scaled = (local_weights.astype(jnp.float32)[..., None] * local_grad.astype(jnp.float32)).astype(
        jnp.bfloat16
    )
    hidden_grad = jnp.einsum(
        "lmd,lfd->lmf",
        local_grad,
        lax.all_gather(down_weight, "dp", axis=1, tiled=True),
        preferred_element_type=jnp.float32,
    ).astype(jnp.bfloat16)
    local_experts = hidden.shape[0]
    shard_rows = down_weight.shape[1]
    part = jnp.einsum("lmf,lmd->fld", hidden, scaled, preferred_element_type=jnp.float32)
    summed = lax.psum_scatter(
        part.reshape(shard_rows * lax.axis_size("dp"), local_experts * width).astype(jnp.bfloat16),
        "dp",
        scatter_dimension=0,
        tiled=True,
    ).astype(jnp.float32)
    down_grad = (
        (summed / replicas)
        .reshape(shard_rows, local_experts, width)
        .transpose(1, 0, 2)
        .astype(jnp.bfloat16)
    )
    expert_pre = swiglu_back(local_pre, local_weights, hidden_grad, units)
    expert_weight = jnp.sum(
        hidden_grad.astype(jnp.float32) * hidden.astype(jnp.float32), axis=-1
    ).astype(jnp.bfloat16)
    back_pre, back_weight = (
        lax.all_to_all(
            restore(expert_pre, sources), "expert", split_axis=0, concat_axis=0, tiled=True
        ),
        lax.all_to_all(
            restore(expert_weight, sources), "expert", split_axis=0, concat_axis=0, tiled=True
        ),
    )
    pre_grad = back_pre.reshape(EXPERTS * CAP, 2 * units)[target]
    weight_grad = back_weight.reshape(EXPERTS * CAP)[target]
    return (
        pre_grad.reshape(tok_rows, top, 2 * units),
        weight_grad.reshape(tok_rows, top),
        down_grad,
    )


def solution(mesh):
    return jax.shard_map(
        body,
        mesh=mesh,
        in_specs=(
            P(("dp", "expert"), None),
            P(("dp", "expert"), None),
            P(("dp", "expert"), None),
            P(("dp", "expert"), None, None),
            P("expert", "dp", None),
        ),
        out_specs=(
            P(("dp", "expert"), None, None),
            P(("dp", "expert"), None),
            P("expert", "dp", None),
        ),
        check_vma=False,
    )
```

profile of v0, /device:TPU:24, one launch (start us, length us, event | category | flops | bytes accessed | tf_op | source)
XLA Modules:
  0.0 573.7 jit_solution(10673067198018662001)
XLA Ops:
  10.7 2.4 scatter_custom_fusion
  14.2 6.8 %gather_fusion = bf16[1024]{0:T(1024)(128)(2,1)S(1)} fusion(bf16[513]{0:T(1024)(128)(2,1)S(1)} %pad_maximum_fusion.1, s32[1024]{0:T(1024)S(1)} %get-tuple-element.15), kind=kCustom, calls=%fused_computation | custom fusion | bytes 8192 | tf_op jit(solution)/shard_map/gather | solution.py:69
  21.7 15.2 %all-to-all-start = ((bf16[16,1,64]{2,1,0:T(2,128)(2,1)}), bf16[16,1,64]{2,1,0:T(2,128)(2,1)S(1)}, u32[]{:S(2)}, u32[]{:S(2)}) async-start(bf16[16,1,64]{2,1,0:T(2,128)(2,1)} %all_to_all.25), calls=%async_computation | async-start | bytes 16384 | tf_op jit(solution)/shard_map/all_to_all | solution.py:81
  37.4 5.6 gather_fusion.2
  43.0 6.2 %all-to-all-done = bf16[16,1,64]{2,1,0:T(2,128)(2,1)S(1)} async-done(((bf16[16,1,64]{2,1,0:T(2,128)(2,1)}), bf16[16,1,64]{2,1,0:T(2,128)(2,1)S(1)}, u32[]{:S(2)}, u32[]{:S(2)}) %all-to-all-start) | async-done | bytes 2080 | tf_op jit(solution)/shard_map/all_to_all | solution.py:81
  49.2 5.9 %all-to-all-start.2 = ((bf16[16,64,1536]{2,1,0:T(8,128)(2,1)}), bf16[16,64,1536]{2,1,0:T(8,128)(2,1)}, u32[]{:S(2)}, u32[]{:S(2)}) async-start(bf16[16,64,1536]{2,1,0:T(8,128)(2,1)} %bitcast.77), calls=%async_computation.2 | async-start | bytes 6291456 | tf_op jit(solution)/shard_map/all_to_all | solution.py:80
  55.3 6.0 %gather_fusion.1 = bf16[1024,2048]{1,0:T(8,128)(2,1)} fusion(bf16[129,2048]{1,0:T(8,128)(2,1)S(1)} %concatenate.21, s32[1024]{0:T(1024)S(1)} %get-tuple-element.16), kind=kCustom, calls=%fused_computation.1 | custom fusion | bytes 8392704 | tf_op jit(solution)/shard_map/gather | solution.py:65
  61.3 133.0 %all-to-all-done.2 = bf16[16,64,1536]{2,1,0:T(8,128)(2,1)} async-done(((bf16[16,64,1536]{2,1,0:T(8,128)(2,1)}), bf16[16,64,1536]{2,1,0:T(8,128)(2,1)}, u32[]{:S(2)}, u32[]{:S(2)}) %all-to-all-start.2) | async-done | bytes 3145760 | tf_op jit(solution)/shard_map/all_to_all | solution.py:80
  194.3 8.2 %all-to-all-start.1 = ((bf16[16,64,2048]{2,1,0:T(8,128)(2,1)}), bf16[16,64,2048]{2,1,0:T(8,128)(2,1)}, u32[]{:S(2)}, u32[]{:S(2)}) async-start(bf16[16,64,2048]{2,1,0:T(8,128)(2,1)} %bitcast.76), calls=%async_computation.1 | async-start | bytes 8388608 | tf_op jit(solution)/shard_map/all_to_all | solution.py:79
  203.4 63.9 %all-gather.2.cloned.1.call-done = bf16[1,768,2048]{2,1,0:T(8,128)(2,1)} async-done(((bf16[1,24,2048]{2,1,0:T(8,128)(2,1)}), bf16[1,768,2048]{2,1,0:T(8,128)(2,1)}) %all-gather.2.cloned.1.call-update) | async-done | bytes 3145744 | tf_op jit(solution)/shard_map/all_gather | solution.py:93
  267.3 117.7 %all-to-all-done.1 = bf16[16,64,2048]{2,1,0:T(8,128)(2,1)} async-done(((bf16[16,64,2048]{2,1,0:T(8,128)(2,1)}), bf16[16,64,2048]{2,1,0:T(8,128)(2,1)}, u32[]{:S(2)}, u32[]{:S(2)}) %all-to-all-start.1) | async-done | bytes 4194336 | tf_op jit(solution)/shard_map/all_to_all | solution.py:79
  385.0 8.6 %fusion.13 = (bf16[1,1024,768]{2,1,0:T(8,128)(2,1)S(1)}, bf16[1,1024,768]{2,1,0:T(8,128)(2,1)S(1)}, bf16[1024]{0:T(1024)(128)(2,1)S(1)}) fusion(f32[1024]{0:T(1024)S(1)} %reshape.213, bf16[1,1024,1536]{2,1,0:T(8,128)(2,1)} %bitcast.8, bf16[1024,2048]{1,0:T(8,128)(2,1)} %bitcast.4, bf16[1,768,2048]{2,1,0:T(8,128)(2,1)} %all-gather.2.cloned.1.call-done), kind=kOutput, calls=%fused_computation.25 | convolution fusion | flops 3240098816 | bytes 13637632 | tf_op jit(solution)/shard_map/lmd,lfd->lmf/dot_general | solution.py:90
  394.3 10.5 %all-to-all-start.4 = ((bf16[16,1,64]{2,1,0:T(2,128)(2,1)}), bf16[16,1,64]{2,1,0:T(2,128)(2,1)S(1)}, u32[]{:S(2)}, u32[]{:S(2)}) async-start(bf16[16,1,64]{2,1,0:T(2,128)(2,1)} %convert_element_type.152), calls=%async_computation.4 | async-start | bytes 16384 | tf_op jit(solution)/shard_map/all_to_all | solution.py:119
  404.8 1.9 pad_maximum_fusion
  406.8 10.4 %all-to-all-done.4 = bf16[16,1,64]{2,1,0:T(2,128)(2,1)S(1)} async-done(((bf16[16,1,64]{2,1,0:T(2,128)(2,1)}), bf16[16,1,64]{2,1,0:T(2,128)(2,1)S(1)}, u32[]{:S(2)}, u32[]{:S(2)}) %all-to-all-start.4) | async-done | bytes 2080 | tf_op jit(solution)/shard_map/all_to_all | solution.py:119
  417.2 3.7 all-to-all-start.3
  421.2 8.9 %fusion.23 = bf16[768,2048]{0,1:T(8,128)(2,1)} fusion(bf16[1,1024,1,1,1,1,2048]{6,1,5,4,3,2,0:T(8,128)(2,1)} %bitcast.21, f32[1024]{0:T(1024)S(1)} %reshape.213, bf16[1,1024,1536]{2,1,0:T(8,128)(2,1)} %bitcast.8), kind=kOutput, calls=%fused_computation.36 | convolution fusion | flops 3235381248 | bytes 10489856 | tf_op jit(solution)/shard_map/lmf,lmd->fld/dot_general | solution.py:98
  430.1 4.8 copy.25
  435.0 3.5 gather_fusion.4
  439.3 99.8 %reduce-scatter.4.cloned.1.call-done = bf16[24,2048]{1,0:T(8,128)(2,1)} async-done(((bf16[768,2048]{1,0:T(8,128)(2,1)}), bf16[24,2048]{1,0:T(8,128)(2,1)}) %reduce-scatter.4.cloned.1.call-update) | async-done | bytes 98320
  541.0 1.9 fusion.30
  544.8 15.3 %all-to-all-done.3 = bf16[16,64,1536]{2,1,0:T(8,128)(2,1)S(1)} async-done(((bf16[16,64,1536]{2,1,0:T(8,128)(2,1)}), bf16[16,64,1536]{2,1,0:T(8,128)(2,1)S(1)}, u32[]{:S(2)}, u32[]{:S(2)}) %all-to-all-start.3) | async-done | bytes 3145760 | tf_op jit(solution)/shard_map/all_to_all | solution.py:116
  560.0 3.0 gather_fusion.3
  563.0 3.8 reshape.209
  (40 shorter events, 12.1 us)
Async XLA Ops:
  7.2 29.7 %copy-start = (bf16[128,4,1536]{2,1,0:T(4,128)(2,1)S(1)}, bf16[128,4,1536]{2,1,0:T(4,128)(2,1)}, u32[]{:S(2)}) copy-start(bf16[128,4,1536]{2,1,0:T(4,128)(2,1)} %param.8) | copy-start | bytes 4718596
  21.7 27.6 %all-to-all-start = ((bf16[16,1,64]{2,1,0:T(2,128)(2,1)}), bf16[16,1,64]{2,1,0:T(2,128)(2,1)S(1)}, u32[]{:S(2)}, u32[]{:S(2)}) async-start(bf16[16,1,64]{2,1,0:T(2,128)(2,1)} %all_to_all.25), calls=%async_computation | async-start | bytes 16384 | tf_op jit(solution)/shard_map/all_to_all | solution.py:81
  49.2 6.0 %copy-start.1 = (bf16[128,2048]{1,0:T(8,128)(2,1)S(1)}, bf16[128,2048]{1,0:T(8,128)(2,1)}, u32[]{:S(2)}) copy-start(bf16[128,2048]{1,0:T(8,128)(2,1)} %param.5) | copy-start | bytes 1572868
  49.2 145.1 %all-to-all-start.2 = ((bf16[16,64,1536]{2,1,0:T(8,128)(2,1)}), bf16[16,64,1536]{2,1,0:T(8,128)(2,1)}, u32[]{:S(2)}, u32[]{:S(2)}) async-start(bf16[16,64,1536]{2,1,0:T(8,128)(2,1)} %bitcast.77), calls=%async_computation.2 | async-start | bytes 6291456 | tf_op jit(solution)/shard_map/all_to_all | solution.py:80
  194.3 190.7 %all-to-all-start.1 = ((bf16[16,64,2048]{2,1,0:T(8,128)(2,1)}), bf16[16,64,2048]{2,1,0:T(8,128)(2,1)}, u32[]{:S(2)}, u32[]{:S(2)}) async-start(bf16[16,64,2048]{2,1,0:T(8,128)(2,1)} %bitcast.76), calls=%async_computation.1 | async-start | bytes 8388608 | tf_op jit(solution)/shard_map/all_to_all | solution.py:79
  202.5 64.7 %all-gather.2.cloned.1.call-start = ((), (), s32[]{:S(2)}) async-start(), calls=%async_computation.6 | async-start | bytes 3244032 | tf_op jit(solution)/shard_map/all_gather | solution.py:93
  394.3 22.9 %all-to-all-start.4 = ((bf16[16,1,64]{2,1,0:T(2,128)(2,1)}), bf16[16,1,64]{2,1,0:T(2,128)(2,1)S(1)}, u32[]{:S(2)}, u32[]{:S(2)}) async-start(bf16[16,1,64]{2,1,0:T(2,128)(2,1)} %convert_element_type.152), calls=%async_computation.4 | async-start | bytes 16384 | tf_op jit(solution)/shard_map/all_to_all | solution.py:119
  417.2 142.8 %all-to-all-start.3 = ((bf16[16,64,1536]{2,1,0:T(8,128)(2,1)}), bf16[16,64,1536]{2,1,0:T(8,128)(2,1)S(1)}, u32[]{:S(2)}, u32[]{:S(2)}) async-start(bf16[16,64,1536]{2,1,0:T(8,128)(2,1)} %pad_maximum_fusion), calls=%async_computation.3 | async-start | bytes 6291456 | tf_op jit(solution)/shard_map/all_to_all | solution.py:116
  421.0 118.1 %reduce-scatter.4.cloned.1.call-start = ((), (), s32[]{:S(2)}) async-start(), calls=%async_computation.7 | async-start | bytes 3244032
Sparse Core Ops, SparseCore 0:
  206.5 60.7 all-gather.1
  435.0 104.0 reduce-scatter.3
where the time goes:
time: 574 us
  waiting for transfers between devices  447 us (78%)
  local copies, waits for them, and re-layouts  45.1 us (8%)
  starting transfers between devices  43.9 us (8%)
  matrix products  17.5 us (3%)
  between operations  14.2 us (2%)
  other arithmetic  5.96 us (1%)
    all_to_all x1, waiting for transfers between devices, body(): lax.all_to_all(send_pre, 'expert', split_axis=0, concat_axis=0, tiled=True)  133 us
    all_to_all x1, waiting for transfers between devices, body(): lax.all_to_all(send_grad, 'expert', split_axis=0, concat_axis=0, tiled=True)  118 us
    unnamed x3, waiting for transfers between devices  100 us
    all_gather x1, waiting for transfers between devices, body(): lax.all_gather(down_weight, 'dp', axis=1, tiled=True)  63.9 us
    all_to_all x1, waiting for transfers between devices, body(): lax.all_to_all(restore(expert_pre, sources), 'expert', split_axis=0, conc...  15.3 us
    all_to_all x1, starting transfers between devices, body(): lax.all_to_all(send_weights, 'expert', split_axis=0, concat_axis=0, tiled...  15.2 us
  transfers between devices with their start and end apart: 7, of which 7 were waited for; matrix products, arithmetic and copies ran while one was open for 7% of the time, Pallas kernels for 0%

commit v1 on v0

v1 whole, which is shorter than its diff:
```python
import jax
import jax.numpy as jnp
from jax import lax
from jax.sharding import PartitionSpec as P

F32 = jnp.float32
BF16 = jnp.bfloat16


def gather_rows(x):
    return lax.all_gather(x, "dp", axis=0, tiled=True)


def body(out_grad, expert_ids, route_weights, pre_activations, down_weight):
    tok, width = out_grad.shape
    top = expert_ids.shape[1]
    units = pre_activations.shape[2] // 2
    ndp = lax.axis_size("dp")
    rows = down_weight.shape[1]
    n_all = ndp * tok

    w_all = lax.all_gather(down_weight, "expert", axis=0, tiled=True)
    experts = w_all.shape[0]
    wcat = w_all.reshape(experts * rows, width)
    og_all = gather_rows(out_grad)
    ids_t = gather_rows(expert_ids).T
    rw_t = gather_rows(route_weights).T.astype(F32)

    gate = pre_activations[..., :units].astype(F32)
    up = pre_activations[..., units:].astype(F32)
    sig = jax.nn.sigmoid(gate)
    hidden = (gate * sig * up).astype(BF16)

    send_h = hidden.reshape(tok, top, ndp, rows).transpose(2, 0, 1, 3)
    got_h = lax.all_to_all(send_h, "dp", 0, 0, tiled=True)
    hid_t = got_h.transpose(2, 3, 0, 1).reshape(top, rows, n_all).astype(F32)

    eidx = jnp.arange(experts, dtype=jnp.int32)[:, None, None]
    hp = jnp.zeros((experts, rows, n_all), F32)
    for k in range(top):
        hp = hp + jnp.where(ids_t[k][None, None, :] == eidx, (rw_t[k][None, :] * hid_t[k])[None], 0.0)
    hp = hp.reshape(experts * rows, n_all).astype(BF16)
    part = lax.dot_general(hp, og_all, (((1,), (0,)), ((), ())), preferred_element_type=F32)

    r_t = lax.dot_general(wcat, og_all, (((1,), (1,)), ((), ())), preferred_element_type=F32)
    r_t = r_t.reshape(experts, rows, n_all)
    hg_t = jnp.stack(
        [jnp.sum(jnp.where(ids_t[k][None, None, :] == eidx, r_t, 0.0), axis=0) for k in range(top)]
    ).astype(BF16)

    send_g = hg_t.reshape(top, rows, ndp, tok).transpose(2, 3, 0, 1)
    got_g = lax.all_to_all(send_g, "dp", 0, 0, tiled=True)
    hidden_grad = got_g.transpose(1, 2, 0, 3).reshape(tok, top, units)

    hg32 = hidden_grad.astype(F32)
    weight_grad = jnp.sum(hg32 * hidden.astype(F32), axis=-1).astype(BF16)
    cot = route_weights.astype(F32)[..., None] * hg32
    gate_grad = cot * up * sig * (1.0 + gate * (1.0 - sig))
    up_grad = cot * gate * sig
    pre_grad = jnp.concatenate([gate_grad, up_grad], axis=-1).astype(BF16)

    summed = lax.psum_scatter(
        part.reshape(experts, rows, width).astype(BF16), "expert", scatter_dimension=0, tiled=True
    )
    down_grad = (summed.astype(F32) / ndp).astype(BF16)
    return pre_grad, weight_grad, down_grad


def solution(mesh):
    return jax.shard_map(
        body,
        mesh=mesh,
        in_specs=(
            P(("dp", "expert"), None),
            P(("dp", "expert"), None),
            P(("dp", "expert"), None),
            P(("dp", "expert"), None, None),
            P("expert", "dp", None),
        ),
        out_specs=(
            P(("dp", "expert"), None, None),
            P(("dp", "expert"), None),
            P("expert", "dp", None),
        ),
        check_vma=False,
    )
```

time: 574 us -> 326 us (0.57)
  waiting for transfers between devices: 447 us -> 208 us
  blocking collectives: 0 us -> 48.3 us
  local copies, waits for them, and re-layouts: 45.1 us -> 10.3 us
  starting transfers between devices: 43.9 us -> 11.9 us
  matrix products: 17.5 us -> 26.4 us
    all_to_all x5 -> x2, waiting for transfers between devices: 283 us -> 24.7 us  [the longest x1 12.5 us: body(): got_g = lax.all_to_all(send_g, 'dp', 0, 0, tiled=True)]
    unnamed x3, waiting for transfers between devices: 100 us -> 1.39 us
    reduce_scatter x0 -> x1, waiting for transfers between devices: none -> 68.6 us  [body(): lax.psum_scatter(part.reshape(experts, rows, width).astype(BF16), 'expert...]
    all_gather x1 -> x2, waiting for transfers between devices: 63.9 us -> 113 us  [the longest x1 87.7 us: gather_rows(): return lax.all_gather(x, 'dp', axis=0, tiled=True)]
    all_gather x0 -> x2, blocking collectives: none -> 48.3 us  [gather_rows(): return lax.all_gather(x, 'dp', axis=0, tiled=True)]
    all_to_all x5 -> x2, starting transfers between devices: 43.6 us -> 11.6 us  [the longest x1 6.03 us: body(): got_g = lax.all_to_all(send_g, 'dp', 0, 0, tiled=True)]
    gather x5 -> x0, local copies, waits for them, and re-layouts: 24.9 us -> none  [the longest x1 6.8 us: body(): send_weights = flat_weights[source].reshape(EXPERTS, CAP)]
    dot_general x2, matrix products: 17.5 us -> 26.4 us  [the longest x1 13.7 us: body(): lax.dot_general(hp, og_all, (((1,), (0,)), ((), ())), preferred_element_t...]
  transfers between devices with their start and end apart: 7 -> 5, of which waited for: 7 -> 5; matrix products, arithmetic and copies ran while one was open for 7% -> 2% of each run, Pallas kernels for 0% -> 0%
where the time goes in v1:
time: 326 us; the launch traced here: 325 us
  waiting for transfers between devices  208 us (64%)
  blocking collectives  48.3 us (15%)
  matrix products  26.4 us (8%)
  between operations  14 us (4%)
  starting transfers between devices  11.9 us (4%)
  local copies, waits for them, and re-layouts  10.3 us (3%)
  other arithmetic  6.07 us (2%)
    all_gather x1, waiting for transfers between devices, gather_rows(): return lax.all_gather(x, 'dp', axis=0, tiled=True)  87.7 us
    reduce_scatter x1, waiting for transfers between devices, body(): lax.psum_scatter(part.reshape(experts, rows, width).astype(BF16), 'expert...  68.6 us
    all_gather x2, blocking collectives, gather_rows(): return lax.all_gather(x, 'dp', axis=0, tiled=True)  48.3 us
    all_gather x1, waiting for transfers between devices, body(): w_all = lax.all_gather(down_weight, 'expert', axis=0, tiled=True)  25.7 us
    dot_general x1, matrix products, body(): lax.dot_general(hp, og_all, (((1,), (0,)), ((), ())), preferred_element_t...  13.7 us
    dot_general x1, matrix products, body(): lax.dot_general(wcat, og_all, (((1,), (1,)), ((), ())), preferred_element...  12.7 us
    all_to_all x1, waiting for transfers between devices, body(): got_g = lax.all_to_all(send_g, 'dp', 0, 0, tiled=True)  12.5 us
    all_to_all x1, waiting for transfers between devices, body(): got_h = lax.all_to_all(send_h, 'dp', 0, 0, tiled=True)  12.2 us
  transfers between devices with their start and end apart: 5, of which 5 were waited for; matrix products, arithmetic and copies ran while one was open for 2% of the time, Pallas kernels for 0%

profile of v1, /device:TPU:24, one launch (start us, length us, event | category | flops | bytes accessed | tf_op | source)
XLA Modules:
  0.0 325.0 jit_solution(932634305599170821)
XLA Ops:
  7.2 0.7 all-gather.3.cloned.1.call-update
  7.9 0.7 all-gather.5.cloned.1.call-update
  8.6 1.9 fusion.30
  10.6 0.7 copy.37
  11.3 0.7 copy.36
  12.0 26.8 %all_gather.15 = bf16[4096,4]{0,1:T(4,128)(2,1)S(1)} all-gather(bf16[128,4]{0,1:T(4,128)(2,1)S(1)} %copy-done.1), channel_id=1, replica_groups=mesh['dp'=32,'expert'=16] {'dp'}, dimensions={0}, use_global_device_ids=true | all-gather | bytes 33792 | tf_op jit(solution)/shard_map/all_gather | solution.py:11
  38.7 21.5 %all_gather.12 = s32[4096,4]{0,1:T(4,128)S(1)} all-gather(s32[128,4]{0,1:T(4,128)S(1)} %copy-done.2), channel_id=1, replica_groups=mesh['dp'=32,'expert'=16] {'dp'}, dimensions={0}, use_global_device_ids=true | all-gather | bytes 67584 | tf_op jit(solution)/shard_map/all_gather | solution.py:11
  60.4 25.7 %all-gather.3.cloned.1.call-done = bf16[16,24,2048]{2,1,0:T(8,128)(2,1)} async-done(((bf16[1,24,2048]{2,1,0:T(8,128)(2,1)}), bf16[16,24,2048]{2,1,0:T(8,128)(2,1)}) %all-gather.3.cloned.1.call-update) | async-done | bytes 1572880 | tf_op jit(solution)/shard_map/all_gather | solution.py:22
  86.1 87.7 %all-gather.5.cloned.1.call-done = bf16[4096,2048]{1,0:T(8,128)(2,1)} async-done(((bf16[128,2048]{1,0:T(8,128)(2,1)}), bf16[4096,2048]{1,0:T(8,128)(2,1)}) %all-gather.5.cloned.1.call-update) | async-done | bytes 16777232 | tf_op jit(solution)/shard_map/all_gather | solution.py:11
  173.8 12.7 %select_reduce_fusion.3 = (bf16[24,4096]{1,0:T(8,128)(2,1)S(1)}, bf16[24,4096]{1,0:T(8,128)(2,1)S(1)}, bf16[24,4096]{1,0:T(8,128)(2,1)S(1)}, bf16[24,4096]{1,0:T(8,128)(2,1)S(1)}) fusion(pred[16,4096]{1,0:T(8,128)(4,1)S(1)} %get-tuple-element.37, pred[16,4096]{1,0:T(8,128)(4,1)S(1)} %get-tuple-element.34, pred[16,4096]{1,0:T(8,128)(4,1)S(1)} %get-tuple-element.35, ...), kind=kOutput, calls=%fused_computation.8 | convolution fusion | flops 6454640640 | bytes 19398656 | tf_op jit(solution)/shard_map/dot_general | solution.py:45
  186.8 1.2 copy.25
  188.0 6.0 %all-to-all-start = ((bf16[32,128,4,24]{1,3,2,0:T(8,128)(2,1)}), bf16[32,128,4,24]{1,3,2,0:T(8,128)(2,1)S(1)}, u32[]{:S(2)}, u32[]{:S(2)}) async-start(bf16[32,128,4,24]{1,3,2,0:T(8,128)(2,1)} %copy.25), calls=%async_computation | async-start | bytes 1572864 | tf_op jit(solution)/shard_map/all_to_all | solution.py:52
  194.1 12.5 %all-to-all-done = bf16[32,128,4,24]{1,3,2,0:T(8,128)(2,1)S(1)} async-done(((bf16[32,128,4,24]{1,3,2,0:T(8,128)(2,1)}), bf16[32,128,4,24]{1,3,2,0:T(8,128)(2,1)S(1)}, u32[]{:S(2)}, u32[]{:S(2)}) %all-to-all-start) | async-done | bytes 786464 | tf_op jit(solution)/shard_map/all_to_all | solution.py:52
  206.5 2.6 fusion.26
  209.2 1.0 copy.29
  210.2 5.5 %all-to-all-start.1 = ((bf16[32,128,4,24]{1,3,2,0:T(8,128)(2,1)}), bf16[32,128,4,24]{1,3,2,0:T(8,128)(2,1)S(1)}, u32[]{:S(2)}, u32[]{:S(2)}) async-start(bf16[32,128,4,24]{1,3,2,0:T(8,128)(2,1)} %copy.29), calls=%async_computation.1 | async-start | bytes 1572864 | tf_op jit(solution)/shard_map/all_to_all | solution.py:35
  216.0 12.2 %all-to-all-done.1 = bf16[32,128,4,24]{1,3,2,0:T(8,128)(2,1)S(1)} async-done(((bf16[32,128,4,24]{1,3,2,0:T(8,128)(2,1)}), bf16[32,128,4,24]{1,3,2,0:T(8,128)(2,1)S(1)}, u32[]{:S(2)}, u32[]{:S(2)}) %all-to-all-start.1) | async-done | bytes 786464 | tf_op jit(solution)/shard_map/all_to_all | solution.py:35
  228.6 0.3 broadcast_multiply_fusion
  229.1 0.3 broadcast_multiply_fusion.1
  230.8 13.7 %fusion.13 = bf16[16,24,2048]{2,1,0:T(8,128)(2,1)} fusion(bf16[4096,2048]{1,0:T(8,128)(2,1)} %all-gather.5.cloned.1.call-done, f32[24,4096]{1,0:T(8,128)S(1)} %bitcast.84, f32[24,4096]{1,0:T(8,128)S(1)} %bitcast.85, f32[24,4096]{1,0:T(8,128)S(1)} %bitcast.86, f32[24,4096]{1,0:T(8,128)S(1)} %bitcast.87, pred[16,4096]{1,0:T(8,128)(4,1)S(1)} %get-tuple-element.34, ...), kind=kOutput, calls=%fused_computation.18 | convolution fusion | flops 6455820288 | bytes 20185088 | tf_op jit(solution)/shard_map/dot_general | solution.py:43
  244.6 1.1 copy-done
  245.8 2.5 copy.31
  248.2 68.6 %reduce-scatter.2.cloned.1.call-done = bf16[1,24,2048]{2,1,0:T(8,128)(2,1)} async-done(((bf16[16,24,2048]{2,1,0:T(8,128)(2,1)}), bf16[1,24,2048]{2,1,0:T(8,128)(2,1)}) %reduce-scatter.2.cloned.1.call-update) | async-done | bytes 98320 | tf_op jit(solution)/shard_map/reduce_scatter | solution.py:62
  316.9 1.6 multiply_convert_fusion
  (29 shorter events, 2.9 us)
Async XLA Ops:
  7.2 79.0 %all-gather.3.cloned.1.call-start = ((), (), s32[]{:S(2)}) async-start(), calls=%async_computation.3 | async-start | bytes 1671168 | tf_op jit(solution)/shard_map/all_gather | solution.py:22
  7.9 165.9 %all-gather.5.cloned.1.call-start = ((), (), s32[]{:S(2)}) async-start(), calls=%async_computation.4 | async-start | bytes 17301504 | tf_op jit(solution)/shard_map/all_gather | solution.py:11
  10.6 1.4 copy-start.1
  10.6 28.1 %copy-start.2 = (s32[128,4]{0,1:T(4,128)S(1)}, s32[128,4]{0,1:T(4,128)}, u32[]{:S(2)}) copy-start(s32[128,4]{0,1:T(4,128)} %param.6) | copy-start | bytes 6148
  188.0 18.5 %all-to-all-start = ((bf16[32,128,4,24]{1,3,2,0:T(8,128)(2,1)}), bf16[32,128,4,24]{1,3,2,0:T(8,128)(2,1)S(1)}, u32[]{:S(2)}, u32[]{:S(2)}) async-start(bf16[32,128,4,24]{1,3,2,0:T(8,128)(2,1)} %copy.25), calls=%async_computation | async-start | bytes 1572864 | tf_op jit(solution)/shard_map/all_to_all | solution.py:52
  210.2 18.0 %all-to-all-start.1 = ((bf16[32,128,4,24]{1,3,2,0:T(8,128)(2,1)}), bf16[32,128,4,24]{1,3,2,0:T(8,128)(2,1)S(1)}, u32[]{:S(2)}, u32[]{:S(2)}) async-start(bf16[32,128,4,24]{1,3,2,0:T(8,128)(2,1)} %copy.29), calls=%async_computation.1 | async-start | bytes 1572864 | tf_op jit(solution)/shard_map/all_to_all | solution.py:35
  215.7 101.2 %reduce-scatter.2.cloned.1.call-start = ((), (), s32[]{:S(2)}) async-start(), calls=%async_computation.5 | async-start | bytes 1671168 | tf_op jit(solution)/shard_map/reduce_scatter | solution.py:62
  244.5 1.1 copy-start
Sparse Core Ops, SparseCore 0:
  10.1 76.0 all-gather.2
  89.3 84.5 all-gather.4
  244.7 72.1 reduce-scatter.1

commit v2 on v1

v2 whole, which is shorter than its diff:
```python
import jax
import jax.numpy as jnp
from jax import lax
from jax.sharding import PartitionSpec as P

F32 = jnp.float32
BF16 = jnp.bfloat16


def body(out_grad, expert_ids, route_weights, pre_activations, down_weight):
    tok, width = out_grad.shape
    top = expert_ids.shape[1]
    units = pre_activations.shape[2] // 2
    ndp = lax.axis_size("dp")
    rows = down_weight.shape[1]
    n_all = ndp * tok

    nex = lax.axis_size("expert")
    w_all = lax.all_to_all(
        jnp.broadcast_to(down_weight, (nex,) + down_weight.shape[1:]), "expert", 0, 0, tiled=True
    )
    experts = w_all.shape[0]
    wcat = w_all.reshape(experts * rows, width)
    og_all = lax.all_gather(out_grad, "dp", axis=0, tiled=True)

    gate = pre_activations[..., :units].astype(F32)
    up = pre_activations[..., units:].astype(F32)
    sig = jax.nn.sigmoid(gate)
    hidden = (gate * sig * up).astype(BF16)

    send_h = hidden.reshape(tok, top, ndp, rows).transpose(2, 1, 3, 0)
    meta = jnp.stack([expert_ids.T.astype(BF16), route_weights.T], axis=1)
    send_h = jnp.concatenate([send_h, jnp.broadcast_to(meta[None], (ndp, top, 2, tok))], axis=2)
    got_h = lax.all_to_all(send_h, "dp", 0, 0, tiled=True)
    got_h = got_h.transpose(1, 2, 0, 3).reshape(top, rows + 2, n_all)
    hid_t = got_h[:, :rows].astype(F32)
    ids_t = got_h[:, rows].astype(F32)
    rw_t = got_h[:, rows + 1].astype(F32)

    eidx = jnp.arange(experts, dtype=F32)[:, None, None]
    hp = jnp.zeros((experts, rows, n_all), F32)
    for k in range(top):
        hp = hp + jnp.where(ids_t[k][None, None, :] == eidx, (rw_t[k][None, :] * hid_t[k])[None], 0.0)
    hp = hp.reshape(experts * rows, n_all).astype(BF16)
    part = lax.dot_general(hp, og_all, (((1,), (0,)), ((), ())), preferred_element_type=F32)
    part = part.reshape(experts, rows, width).astype(BF16)
    part, wcat = lax.optimization_barrier((part, wcat))

    r_t = lax.dot_general(wcat, og_all, (((1,), (1,)), ((), ())), preferred_element_type=F32)
    r_t = r_t.reshape(experts, rows, n_all)
    hg_t = jnp.stack(
        [jnp.sum(jnp.where(ids_t[k][None, None, :] == eidx, r_t, 0.0), axis=0) for k in range(top)]
    ).astype(BF16)

    send_g = hg_t.reshape(top, rows, ndp, tok).transpose(2, 0, 1, 3)
    got_g = lax.all_to_all(send_g, "dp", 0, 0, tiled=True)
    hidden_grad = got_g.transpose(3, 1, 0, 2).reshape(tok, top, units)

    hg32 = hidden_grad.astype(F32)
    weight_grad = jnp.sum(hg32 * hidden.astype(F32), axis=-1).astype(BF16)
    cot = route_weights.astype(F32)[..., None] * hg32
    gate_grad = cot * up * sig * (1.0 + gate * (1.0 - sig))
    up_grad = cot * gate * sig
    pre_grad = jnp.concatenate([gate_grad, up_grad], axis=-1).astype(BF16)

    summed = lax.psum_scatter(part, "expert", scatter_dimension=0, tiled=True)
    down_grad = (summed.astype(F32) / ndp).astype(BF16)
    return pre_grad, weight_grad, down_grad


def solution(mesh):
    return jax.shard_map(
        body,
        mesh=mesh,
        in_specs=(
            P(("dp", "expert"), None),
            P(("dp", "expert"), None),
            P(("dp", "expert"), None),
            P(("dp", "expert"), None, None),
            P("expert", "dp", None),
        ),
        out_specs=(
            P(("dp", "expert"), None, None),
            P(("dp", "expert"), None),
            P("expert", "dp", None),
        ),
        check_vma=False,
    )
```

time: 326 us -> 199 us (0.61)
  waiting for transfers between devices: 208 us -> 92.6 us
  blocking collectives: 48.3 us -> 21.5 us
  starting transfers between devices: 11.9 us -> 22.3 us
  other arithmetic: 6.07 us -> 12 us
    all_gather x2 -> x1, waiting for transfers between devices: 113 us -> 46.4 us  [body(): og_all = lax.all_gather(out_grad, 'dp', axis=0, tiled=True)]
    all_gather x2 -> x0, blocking collectives: 48.3 us -> none  [gather_rows(): return lax.all_gather(x, 'dp', axis=0, tiled=True)]
    reduce_scatter x1, waiting for transfers between devices: 68.6 us -> 28.6 us  [body(): summed = lax.psum_scatter(part, 'expert', scatter_dimension=0, tiled=True)]
    all_to_all x0 -> x1, blocking collectives: none -> 21.5 us  [body(): got_h = lax.all_to_all(send_h, 'dp', 0, 0, tiled=True)]
    all_to_all x1, starting transfers between devices: 5.54 us -> 14 us  [body(): lax.all_to_all(jnp.broadcast_to(down_weight, (nex,) + down_weight.shape[1...]
    all_to_all x1, waiting for transfers between devices: 12.2 us -> 4.51 us  [body(): lax.all_to_all(jnp.broadcast_to(down_weight, (nex,) + down_weight.shape[1...]
  transfers between devices with their start and end apart: 5 -> 4, of which waited for: 5 -> 4; matrix products, arithmetic and copies ran while one was open for 2% -> 23% of each run, Pallas kernels for 0% -> 0%
where the time goes in v2:
time: 199 us
  waiting for transfers between devices  92.6 us (47%)
  matrix products  24.5 us (12%)
  starting transfers between devices  22.3 us (11%)
  blocking collectives  21.5 us (11%)
  between operations  14.4 us (7%)
  other arithmetic  12 us (6%)
  local copies, waits for them, and re-layouts  11.3 us (6%)
    all_gather x1, waiting for transfers between devices, body(): og_all = lax.all_gather(out_grad, 'dp', axis=0, tiled=True)  46.4 us
    reduce_scatter x1, waiting for transfers between devices, body(): summed = lax.psum_scatter(part, 'expert', scatter_dimension=0, tiled=True)  28.6 us
    all_to_all x1, blocking collectives, body(): got_h = lax.all_to_all(send_h, 'dp', 0, 0, tiled=True)  21.5 us
    all_to_all x1, starting transfers between devices, body(): lax.all_to_all(jnp.broadcast_to(down_weight, (nex,) + down_weight.shape[1...  14 us
    dot_general x1, matrix products, body(): lax.dot_general(hp, og_all, (((1,), (0,)), ((), ())), preferred_element_t...  13.7 us
    all_to_all x1, waiting for transfers between devices, body(): got_g = lax.all_to_all(send_g, 'dp', 0, 0, tiled=True)  12.5 us
    dot_general x1, matrix products, body(): lax.dot_general(wcat, og_all, (((1,), (1,)), ((), ())), preferred_element...  10.8 us
    all_to_all x1, starting transfers between devices, body(): got_g = lax.all_to_all(send_g, 'dp', 0, 0, tiled=True)  8.21 us
  transfers between devices with their start and end apart: 4, of which 4 were waited for; matrix products, arithmetic and copies ran while one was open for 23% of the time, Pallas kernels for 0%

profile of v2, /device:TPU:24, one launch (start us, length us, event | category | flops | bytes accessed | tf_op | source)
XLA Modules:
  0.0 198.5 jit_solution(6629555992069582197)
XLA Ops:
  7.2 0.7 all-gather.2.cloned.1.call-update
  7.9 1.9 fusion.26
  9.8 0.7 copy.28
  10.5 0.7 copy.29
  12.6 21.5 %all_to_all.15 = bf16[32,4,26,128]{3,1,2,0:T(4,128)(2,1)S(1)} all-to-all(bf16[32,4,26,128]{3,1,2,0:T(4,128)(2,1)S(1)} %copy.19), channel_id=1, replica_groups=mesh['dp'=32,'expert'=16] {'dp'}, dimensions={0} | all-to-all | bytes 1703936 | tf_op jit(solution)/shard_map/all_to_all | solution.py:34
  34.1 1.3 broadcast_in_dim.115
  35.5 14.0 %all-to-all-start.1 = ((bf16[16,24,2048]{2,1,0:T(8,128)(2,1)}), bf16[16,24,2048]{2,1,0:T(8,128)(2,1)}, u32[]{:S(2)}, u32[]{:S(2)}) async-start(bf16[16,24,2048]{2,1,0:T(8,128)(2,1)} %broadcast_in_dim.115), calls=%async_computation.1 | async-start | bytes 3145728 | tf_op jit(solution)/shard_map/all_to_all | solution.py:19
  50.3 1.8 slice_multiply_fusion.3
  52.8 1.0 copy.46
  53.8 0.7 iota_compare_fusion
  54.4 0.7 iota_compare_fusion.1
  55.7 0.7 iota_compare_fusion.3
  56.4 46.4 %all-gather.2.cloned.1.call-done = bf16[4096,2048]{1,0:T(8,128)(2,1)} async-done(((bf16[128,2048]{1,0:T(8,128)(2,1)}), bf16[4096,2048]{1,0:T(8,128)(2,1)}) %all-gather.2.cloned.1.call-update) | async-done | bytes 16777232 | tf_op jit(solution)/shard_map/all_gather | solution.py:24
  102.8 13.7 %fusion.11 = bf16[16,24,2048]{2,1,0:T(8,128)(2,1)} fusion(bf16[4096,2048]{1,0:T(8,128)(2,1)} %all-gather.2.cloned.1.call-done, f32[24,4096]{1,0:T(8,128)S(1)} %bitcast.89, f32[24,4096]{1,0:T(8,128)S(1)} %bitcast.90, f32[24,4096]{1,0:T(8,128)S(1)} %bitcast.91, f32[24,4096]{1,0:T(8,128)} %bitcast.92, pred[16,4096]{1,0:T(8,128)(4,1)} %iota_compare_fusion, ...), kind=kOutput, calls=%fused_computation.16 | convolution fusion | flops 6455820288 | bytes 20185088 | tf_op jit(solution)/shard_map/dot_general | solution.py:45
  116.5 4.5 %all-to-all-done.1 = bf16[16,24,2048]{2,1,0:T(8,128)(2,1)} async-done(((bf16[16,24,2048]{2,1,0:T(8,128)(2,1)}), bf16[16,24,2048]{2,1,0:T(8,128)(2,1)}, u32[]{:S(2)}, u32[]{:S(2)}) %all-to-all-start.1) | async-done | bytes 1572896 | tf_op jit(solution)/shard_map/all_to_all | solution.py:19
  121.0 10.8 %fusion.29 = f32[384,4096]{1,0:T(8,128)S(1)} fusion(bf16[384,2048]{1,0:T(8,128)(2,1)} %bitcast.17, bf16[4096,2048]{1,0:T(8,128)(2,1)} %all-gather.2.cloned.1.call-done), kind=kOutput, calls=%fused_computation.66 | convolution fusion | flops 6442450944 | bytes 24641536 | tf_op jit(solution)/shard_map/dot_general | solution.py:49
  131.9 3.4 %select_reduce_fusion.3 = (bf16[24,4096]{1,0:T(8,128)(2,1)S(1)}, bf16[24,4096]{1,0:T(8,128)(2,1)S(1)}, bf16[24,4096]{1,0:T(8,128)(2,1)S(1)}, bf16[24,4096]{1,0:T(8,128)(2,1)S(1)}) fusion(f32[16,24,4096]{2,1,0:T(8,128)S(1)} %bitcast.80, pred[16,4096]{1,0:T(8,128)(4,1)S(1)} %copy-done.3, pred[16,4096]{1,0:T(8,128)(4,1)S(1)} %copy-done, ...), kind=kLoop, calls=%fused_computation.5 | loop fusion | flops 12189696 | bytes 7340032 | tf_op jit(solution)/shard_map/reduce_sum | solution.py:52
  135.5 1.2 copy.21
  136.7 8.2 %all-to-all-start.2 = ((bf16[32,4,24,128]{3,2,1,0:T(8,128)(2,1)}), bf16[32,4,24,128]{3,2,1,0:T(8,128)(2,1)S(1)}, u32[]{:S(2)}, u32[]{:S(2)}) async-start(bf16[32,4,24,128]{3,2,1,0:T(8,128)(2,1)} %copy.21), calls=%async_computation.2 | async-start | bytes 1572864 | tf_op jit(solution)/shard_map/all_to_all | solution.py:56
  144.9 12.5 %all-to-all-done.2 = bf16[32,4,24,128]{3,2,1,0:T(8,128)(2,1)S(1)} async-done(((bf16[32,4,24,128]{3,2,1,0:T(8,128)(2,1)}), bf16[32,4,24,128]{3,2,1,0:T(8,128)(2,1)S(1)}, u32[]{:S(2)}, u32[]{:S(2)}) %all-to-all-start.2) | async-done | bytes 786464 | tf_op jit(solution)/shard_map/all_to_all | solution.py:56
  157.4 1.6 fusion.17
  159.1 2.5 %copy.23 = bf16[128,4,1536]{2,1,0:T(4,128)(2,1)} copy(bf16[128,4,1536]{0,2,1:T(8,128)(2,1)S(1)} %pad_maximum_fusion) | data formatting | bytes 3145728
  161.6 28.6 %reduce-scatter.2.cloned.1.call-done = bf16[1,24,2048]{2,1,0:T(8,128)(2,1)} async-done(((bf16[16,24,2048]{2,1,0:T(8,128)(2,1)}), bf16[1,24,2048]{2,1,0:T(8,128)(2,1)}) %reduce-scatter.2.cloned.1.call-update) | async-done | bytes 98320 | tf_op jit(solution)/shard_map/reduce_scatter | solution.py:66
  190.2 1.6 multiply_convert_fusion
  (39 shorter events, 3.8 us)
Async XLA Ops:
  7.2 95.6 %all-gather.2.cloned.1.call-start = ((), (), s32[]{:S(2)}) async-start(), calls=%async_computation.4 | async-start | bytes 17301504 | tf_op jit(solution)/shard_map/all_gather | solution.py:24
  9.8 1.4 copy-start.6
  9.8 1.4 copy-start.5
  11.9 22.2 %copy-start.4 = (bf16[1,24,2048]{2,1,0:T(8,128)(2,1)S(1)}, bf16[1,24,2048]{2,1,0:T(8,128)(2,1)}, u32[]{:S(2)}) copy-start(bf16[1,24,2048]{2,1,0:T(8,128)(2,1)} %param.9) | copy-start | bytes 294916
  35.5 85.5 %all-to-all-start.1 = ((bf16[16,24,2048]{2,1,0:T(8,128)(2,1)}), bf16[16,24,2048]{2,1,0:T(8,128)(2,1)}, u32[]{:S(2)}, u32[]{:S(2)}) async-start(bf16[16,24,2048]{2,1,0:T(8,128)(2,1)} %broadcast_in_dim.115), calls=%async_computation.1 | async-start | bytes 3145728 | tf_op jit(solution)/shard_map/all_to_all | solution.py:19
  49.5 140.7 %reduce-scatter.2.cloned.1.call-start = ((), (), s32[]{:S(2)}) async-start(), calls=%async_computation.5 | async-start | bytes 1671168 | tf_op jit(solution)/shard_map/reduce_scatter | solution.py:66
  121.0 10.8 %copy-start = (pred[16,4096]{1,0:T(8,128)(4,1)S(1)}, pred[16,4096]{1,0:T(8,128)(4,1)}, u32[]{:S(2)}) copy-start(pred[16,4096]{1,0:T(8,128)(4,1)} %iota_compare_fusion) | copy-start | bytes 196612
  121.0 10.8 %copy-start.1 = (pred[16,4096]{1,0:T(8,128)(4,1)S(1)}, pred[16,4096]{1,0:T(8,128)(4,1)}, u32[]{:S(2)}) copy-start(pred[16,4096]{1,0:T(8,128)(4,1)} %iota_compare_fusion.1) | copy-start | bytes 196612
  121.0 10.8 %copy-start.2 = (pred[16,4096]{1,0:T(8,128)(4,1)S(1)}, pred[16,4096]{1,0:T(8,128)(4,1)}, u32[]{:S(2)}) copy-start(pred[16,4096]{1,0:T(8,128)(4,1)} %iota_compare_fusion.2) | copy-start | bytes 196612
  121.0 10.8 %copy-start.3 = (pred[16,4096]{1,0:T(8,128)(4,1)S(1)}, pred[16,4096]{1,0:T(8,128)(4,1)}, u32[]{:S(2)}) copy-start(pred[16,4096]{1,0:T(8,128)(4,1)} %iota_compare_fusion.3) | copy-start | bytes 196612
  136.7 20.7 %all-to-all-start.2 = ((bf16[32,4,24,128]{3,2,1,0:T(8,128)(2,1)}), bf16[32,4,24,128]{3,2,1,0:T(8,128)(2,1)S(1)}, u32[]{:S(2)}, u32[]{:S(2)}) async-start(bf16[32,4,24,128]{3,2,1,0:T(8,128)(2,1)} %copy.21), calls=%async_computation.2 | async-start | bytes 1572864 | tf_op jit(solution)/shard_map/all_to_all | solution.py:56
Sparse Core Ops, SparseCore 0:
  11.1 91.6 all-gather.1
  121.1 68.9 reduce-scatter.1

commit v3 on v2

--- a/solution.py
+++ b/solution.py
@@ -3,11 +3,12 @@
 from jax import lax
 from jax.sharding import PartitionSpec as P
 
+
 F32 = jnp.float32
 BF16 = jnp.bfloat16
 
 
-def body(out_grad, expert_ids, route_weights, pre_activations, down_weight):
+def layer(out_grad, expert_ids, route_weights, pre_activations, down_weight):
     tok, width = out_grad.shape
     top = expert_ids.shape[1]
     units = pre_activations.shape[2] // 2
@@ -46,6 +47,10 @@
     part = part.reshape(experts, rows, width).astype(BF16)
     part, wcat = lax.optimization_barrier((part, wcat))
 
+    split = rows // 2
+    moved = lax.all_to_all(part[:, :split], "expert", 0, 0, tiled=True)
+    second = lax.psum_scatter(part[:, split:], "expert", scatter_dimension=0, tiled=True)
+
     r_t = lax.dot_general(wcat, og_all, (((1,), (1,)), ((), ())), preferred_element_type=F32)
     r_t = r_t.reshape(experts, rows, n_all)
     hg_t = jnp.stack(
@@ -63,14 +68,14 @@
     up_grad = cot * gate * sig
     pre_grad = jnp.concatenate([gate_grad, up_grad], axis=-1).astype(BF16)
 
-    summed = lax.psum_scatter(part, "expert", scatter_dimension=0, tiled=True)
-    down_grad = (summed.astype(F32) / ndp).astype(BF16)
+    first = jnp.sum(moved.astype(F32), axis=0, keepdims=True)
+    down_grad = (jnp.concatenate([first, second.astype(F32)], axis=1) / ndp).astype(BF16)
     return pre_grad, weight_grad, down_grad
 
 
 def solution(mesh):
     return jax.shard_map(
-        body,
+        layer,
         mesh=mesh,
         in_specs=(
             P(("dp", "expert"), None),

time: 199 us -> 262 us (1.32); the launches traced: 199 us -> 259 us
  waiting for transfers between devices: 92.6 us -> 140 us
  starting transfers between devices: 22.3 us -> 29.1 us
  local copies, waits for them, and re-layouts: 11.3 us -> 15.5 us
    reduce_scatter x1, waiting for transfers between devices: 28.6 us -> 79 us  [layer(): lax.psum_scatter(part[:, split:], 'expert', scatter_dimension=0, tiled=True)]
    all_to_all x2 -> x3, starting transfers between devices: 22.2 us -> 29 us  [the longest x1 14 us: layer(): lax.all_to_all(jnp.broadcast_to(down_weight, (nex,) + down_weight.shape[1...]
    slice x2 -> x3, local copies, waits for them, and re-layouts: 2.01 us -> 5.33 us  [the longest x1 3.32 us: layer(): moved = lax.all_to_all(part[:, :split], 'expert', 0, 0, tiled=True)]
    all_to_all x2 -> x3, waiting for transfers between devices: 17 us -> 13.7 us  [the longest x1 9.17 us: layer(): got_g = lax.all_to_all(send_g, 'dp', 0, 0, tiled=True)]
    unnamed x25 -> x27, local copies, waits for them, and re-layouts: 5.62 us -> 6.49 us
  transfers between devices with their start and end apart: 4 -> 5, of which waited for: 4 -> 4; matrix products, arithmetic and copies ran while one was open for 23% -> 14% of each run, Pallas kernels for 0% -> 0%
where the time goes in v3:
time: 262 us; the launch traced here: 259 us
  waiting for transfers between devices  140 us (53%)
  starting transfers between devices  29.1 us (11%)
  matrix products  24.4 us (9%)
  blocking collectives  21.5 us (8%)
  local copies, waits for them, and re-layouts  15.5 us (6%)
  between operations  14.4 us (5%)
  other arithmetic  13.5 us (5%)
    reduce_scatter x1, waiting for transfers between devices, layer(): lax.psum_scatter(part[:, split:], 'expert', scatter_dimension=0, tiled=True)  79 us
    all_gather x1, waiting for transfers between devices, layer(): og_all = lax.all_gather(out_grad, 'dp', axis=0, tiled=True)  46.4 us
    all_to_all x1, blocking collectives, layer(): got_h = lax.all_to_all(send_h, 'dp', 0, 0, tiled=True)  21.5 us
    all_to_all x1, starting transfers between devices, layer(): lax.all_to_all(jnp.broadcast_to(down_weight, (nex,) + down_weight.shape[1...  14 us
    dot_general x1, matrix products, layer(): lax.dot_general(hp, og_all, (((1,), (0,)), ((), ())), preferred_element_t...  13.7 us
    dot_general x1, matrix products, layer(): lax.dot_general(wcat, og_all, (((1,), (1,)), ((), ())), preferred_element...  10.8 us
    all_to_all x1, waiting for transfers between devices, layer(): got_g = lax.all_to_all(send_g, 'dp', 0, 0, tiled=True)  9.17 us
    all_to_all x1, starting transfers between devices, layer(): got_g = lax.all_to_all(send_g, 'dp', 0, 0, tiled=True)  8.2 us
  transfers between devices with their start and end apart: 5, of which 4 were waited for; matrix products, arithmetic and copies ran while one was open for 14% of the time, Pallas kernels for 0%

profile of v3, /device:TPU:24, one launch (start us, length us, event | category | flops | bytes accessed | tf_op | source)
XLA Modules:
  0.0 258.9 jit_solution(11099232258070119255)
XLA Ops:
  7.2 0.7 all-gather.2.cloned.1.call-update
  7.9 1.9 fusion.28
  12.6 21.5 %all_to_all.20 = bf16[32,4,26,128]{3,1,2,0:T(4,128)(2,1)S(1)} all-to-all(bf16[32,4,26,128]{3,1,2,0:T(4,128)(2,1)S(1)} %copy.19), channel_id=1, replica_groups=mesh['dp'=32,'expert'=16] {'dp'}, dimensions={0} | all-to-all | bytes 1703936 | tf_op jit(solution)/shard_map/all_to_all | solution.py:35
  34.1 1.3 broadcast_in_dim.116
  35.5 14.0 %all-to-all-start.1 = ((bf16[16,24,2048]{2,1,0:T(8,128)(2,1)}), bf16[16,24,2048]{2,1,0:T(8,128)(2,1)}, u32[]{:S(2)}, u32[]{:S(2)}) async-start(bf16[16,24,2048]{2,1,0:T(8,128)(2,1)} %broadcast_in_dim.116), calls=%async_computation.1 | async-start | bytes 3145728 | tf_op jit(solution)/shard_map/all_to_all | solution.py:20
  50.2 1.8 slice_multiply_fusion.3
  52.7 1.0 copy.46
  55.0 0.7 iota_compare_fusion.2
  56.4 46.4 %all-gather.2.cloned.1.call-done = bf16[4096,2048]{1,0:T(8,128)(2,1)} async-done(((bf16[128,2048]{1,0:T(8,128)(2,1)}), bf16[4096,2048]{1,0:T(8,128)(2,1)}) %all-gather.2.cloned.1.call-update) | async-done | bytes 16777232 | tf_op jit(solution)/shard_map/all_gather | solution.py:25
  102.8 13.7 %fusion.11 = bf16[16,24,2048]{2,1,0:T(8,128)(2,1)} fusion(bf16[4096,2048]{1,0:T(8,128)(2,1)} %all-gather.2.cloned.1.call-done, f32[24,4096]{1,0:T(8,128)S(1)} %bitcast.91, f32[24,4096]{1,0:T(8,128)S(1)} %bitcast.92, f32[24,4096]{1,0:T(8,128)S(1)} %bitcast.93, f32[24,4096]{1,0:T(8,128)} %bitcast.94, pred[16,4096]{1,0:T(8,128)(4,1)} %iota_compare_fusion, ...), kind=kOutput, calls=%fused_computation.16 | convolution fusion | flops 6455820288 | bytes 20185088 | tf_op jit(solution)/shard_map/dot_general | solution.py:46
  116.5 4.5 %all-to-all-done.1 = bf16[16,24,2048]{2,1,0:T(8,128)(2,1)} async-done(((bf16[16,24,2048]{2,1,0:T(8,128)(2,1)}), bf16[16,24,2048]{2,1,0:T(8,128)(2,1)}, u32[]{:S(2)}, u32[]{:S(2)}) %all-to-all-start.1) | async-done | bytes 1572896 | tf_op jit(solution)/shard_map/all_to_all | solution.py:20
  121.0 10.8 %fusion.31 = f32[384,4096]{1,0:T(8,128)S(1)} fusion(bf16[384,2048]{1,0:T(8,128)(2,1)} %bitcast.17, bf16[4096,2048]{1,0:T(8,128)(2,1)} %all-gather.2.cloned.1.call-done), kind=kOutput, calls=%fused_computation.69 | convolution fusion | flops 6442450944 | bytes 24641536 | tf_op jit(solution)/shard_map/dot_general | solution.py:54
  131.8 3.6 %select_reduce_fusion.3 = (bf16[24,4096]{1,0:T(8,128)(2,1)S(1)}, bf16[24,4096]{1,0:T(8,128)(2,1)S(1)}, bf16[24,4096]{1,0:T(8,128)(2,1)S(1)}, bf16[24,4096]{1,0:T(8,128)(2,1)S(1)}) fusion(f32[16,24,4096]{2,1,0:T(8,128)S(1)} %bitcast.81, pred[16,4096]{1,0:T(8,128)(4,1)S(1)} %copy-done.4, pred[16,4096]{1,0:T(8,128)(4,1)S(1)} %copy-done.1, ...), kind=kLoop, calls=%fused_computation.5 | loop fusion | flops 12189696 | bytes 7340032 | tf_op jit(solution)/shard_map/reduce_sum | solution.py:57
  135.6 1.2 copy.21
  136.8 8.2 %all-to-all-start.2 = ((bf16[32,4,24,128]{3,2,1,0:T(8,128)(2,1)}), bf16[32,4,24,128]{3,2,1,0:T(8,128)(2,1)S(1)}, u32[]{:S(2)}, u32[]{:S(2)}) async-start(bf16[32,4,24,128]{3,2,1,0:T(8,128)(2,1)} %copy.21), calls=%async_computation.2 | async-start | bytes 1572864 | tf_op jit(solution)/shard_map/all_to_all | solution.py:61
  145.0 3.3 %fusion.27 = (bf16[16,12,2048]{2,1,0:T(8,128)(2,1)}, bf16[16,12,2048]{2,1,0:T(8,128)(2,1)}) fusion(bf16[16,24,2048]{2,1,0:T(8,128)(2,1)} %fusion.11), kind=kLoop, calls=%fused_computation.65 | loop fusion | bytes 3145728 | tf_op jit(solution)/shard_map/slice | solution.py:51
  148.3 9.2 %all-to-all-done.2 = bf16[32,4,24,128]{3,2,1,0:T(8,128)(2,1)S(1)} async-done(((bf16[32,4,24,128]{3,2,1,0:T(8,128)(2,1)}), bf16[32,4,24,128]{3,2,1,0:T(8,128)(2,1)S(1)}, u32[]{:S(2)}, u32[]{:S(2)}) %all-to-all-start.2) | async-done | bytes 786464 | tf_op jit(solution)/shard_map/all_to_all | solution.py:61
  157.5 0.9 copy-done
  158.4 6.8 %all-to-all-start.3 = ((bf16[16,12,2048]{2,1,0:T(8,128)(2,1)}), bf16[16,12,2048]{2,1,0:T(8,128)(2,1)S(1)}, u32[]{:S(2)}, u32[]{:S(2)}) async-start(bf16[16,12,2048]{2,1,0:T(8,128)(2,1)} %get-tuple-element.19), calls=%async_computation.3 | async-start | bytes 2097152 | tf_op jit(solution)/shard_map/all_to_all | solution.py:51
  165.2 0.7 reduce-scatter.2.cloned.1.call-update
  166.0 2.8 %fusion.17 = (bf16[128,4,768]{0,2,1:T(8,128)(2,1)S(1)}, bf16[128,4,768]{0,2,1:T(8,128)(2,1)S(1)}, bf16[128,4]{0,1:T(4,128)(2,1)}) fusion(bf16[128,4,768]{0,2,1:T(8,128)(2,1)S(1)} %copy.29, bf16[128,4,768]{0,2,1:T(8,128)(2,1)S(1)} %copy.28, f32[128,4]{0,1:T(4,128)S(1)} %convert_element_type.71, bf16[32,4,24,128]{3,2,1,0:T(8,128)(2,1)} %copy-done, ...), kind=kLoop, calls=%fused_computation.27 | loop fusion | flops 7863808 | bytes 4721664 | tf_op jit(solution)/shard_map/convert.2
  168.8 2.5 copy.23
  171.3 79.0 %reduce-scatter.2.cloned.1.call-done = bf16[1,12,2048]{2,1,0:T(8,128)(2,1)} async-done(((bf16[16,12,2048]{2,1,0:T(8,128)(2,1)}), bf16[1,12,2048]{2,1,0:T(8,128)(2,1)}) %reduce-scatter.2.cloned.1.call-update) | async-done | bytes 49168 | tf_op jit(solution)/shard_map/reduce_scatter | solution.py:52
  250.3 0.8 convert_element_type.88
  (46 shorter events, 7.4 us)
Async XLA Ops:
  7.2 95.6 %all-gather.2.cloned.1.call-start = ((), (), s32[]{:S(2)}) async-start(), calls=%async_computation.5 | async-start | bytes 17301504 | tf_op jit(solution)/shard_map/all_gather | solution.py:25
  9.8 1.4 copy-start.7
  9.8 1.4 copy-start.6
  11.9 22.2 %copy-start.5 = (bf16[1,24,2048]{2,1,0:T(8,128)(2,1)S(1)}, bf16[1,24,2048]{2,1,0:T(8,128)(2,1)}, u32[]{:S(2)}) copy-start(bf16[1,24,2048]{2,1,0:T(8,128)(2,1)} %param.9) | copy-start | bytes 294916
  35.5 85.5 %all-to-all-start.1 = ((bf16[16,24,2048]{2,1,0:T(8,128)(2,1)}), bf16[16,24,2048]{2,1,0:T(8,128)(2,1)}, u32[]{:S(2)}, u32[]{:S(2)}) async-start(bf16[16,24,2048]{2,1,0:T(8,128)(2,1)} %broadcast_in_dim.116), calls=%async_computation.1 | async-start | bytes 3145728 | tf_op jit(solution)/shard_map/all_to_all | solution.py:20
  121.0 10.8 %copy-start.1 = (pred[16,4096]{1,0:T(8,128)(4,1)S(1)}, pred[16,4096]{1,0:T(8,128)(4,1)}, u32[]{:S(2)}) copy-start(pred[16,4096]{1,0:T(8,128)(4,1)} %iota_compare_fusion) | copy-start | bytes 196612
  121.0 10.8 %copy-start.2 = (pred[16,4096]{1,0:T(8,128)(4,1)S(1)}, pred[16,4096]{1,0:T(8,128)(4,1)}, u32[]{:S(2)}) copy-start(pred[16,4096]{1,0:T(8,128)(4,1)} %iota_compare_fusion.1) | copy-start | bytes 196612
  121.0 10.8 %copy-start.3 = (pred[16,4096]{1,0:T(8,128)(4,1)S(1)}, pred[16,4096]{1,0:T(8,128)(4,1)}, u32[]{:S(2)}) copy-start(pred[16,4096]{1,0:T(8,128)(4,1)} %iota_compare_fusion.2) | copy-start | bytes 196612
  121.0 10.8 %copy-start.4 = (pred[16,4096]{1,0:T(8,128)(4,1)S(1)}, pred[16,4096]{1,0:T(8,128)(4,1)}, u32[]{:S(2)}) copy-start(pred[16,4096]{1,0:T(8,128)(4,1)} %iota_compare_fusion.3) | copy-start | bytes 196612
  136.8 20.7 %all-to-all-start.2 = ((bf16[32,4,24,128]{3,2,1,0:T(8,128)(2,1)}), bf16[32,4,24,128]{3,2,1,0:T(8,128)(2,1)S(1)}, u32[]{:S(2)}, u32[]{:S(2)}) async-start(bf16[32,4,24,128]{3,2,1,0:T(8,128)(2,1)} %copy.21), calls=%async_computation.2 | async-start | bytes 1572864 | tf_op jit(solution)/shard_map/all_to_all | solution.py:61
  157.5 0.9 copy-start
  158.4 92.8 %all-to-all-start.3 = ((bf16[16,12,2048]{2,1,0:T(8,128)(2,1)}), bf16[16,12,2048]{2,1,0:T(8,128)(2,1)S(1)}, u32[]{:S(2)}, u32[]{:S(2)}) async-start(bf16[16,12,2048]{2,1,0:T(8,128)(2,1)} %get-tuple-element.19), calls=%async_computation.3 | async-start | bytes 2097152 | tf_op jit(solution)/shard_map/all_to_all | solution.py:51
  165.2 85.1 %reduce-scatter.2.cloned.1.call-start = ((), (), s32[]{:S(2)}) async-start(), calls=%async_computation.6 | async-start | bytes 1114112 | tf_op jit(solution)/shard_map/reduce_scatter | solution.py:52
Sparse Core Ops, SparseCore 0:
  11.1 91.6 all-gather.1
  168.8 81.4 reduce-scatter.1

commit v4 on v2

--- a/solution.py
+++ b/solution.py
@@ -1,10 +1,75 @@
 import jax
+import numpy as np
 import jax.numpy as jnp
 from jax import lax
 from jax.sharding import PartitionSpec as P
 
 F32 = jnp.float32
 BF16 = jnp.bfloat16
+SIDE = 4
+
+
+def coords(i):
+    return i // (2 * SIDE), (i // 2) % SIDE, i % 2
+
+
+def index_of(x, y, c):
+    return (x % SIDE) * 2 * SIDE + (y % SIDE) * 2 + c
+
+
+def shift_first(n, s):
+    pairs = []
+    for i in range(n):
+        x, y, c = coords(i)
+        pairs.append((i, index_of(x + s, y, c) if c == 0 else index_of(x, y + s, c)))
+    return pairs
+
+
+def shift_second(n, s):
+    pairs = []
+    for i in range(n):
+        x, y, c = coords(i)
+        pairs.append((i, index_of(x, y + s, c) if c == 0 else index_of(x + s, y, c)))
+    return pairs
+
+
+def ring_gather(block, n):
+    half = block.shape[1] // 2
+    up, down = shift_first(n, 1), shift_first(n, -1)
+    from_low = lax.ppermute(block, "dp", up)
+    from_high = lax.ppermute(block, "dp", down)
+    far_left = lax.ppermute(from_low[:, :half], "dp", up)
+    far_right = lax.ppermute(from_high[:, half:], "dp", down)
+    line = jnp.concatenate(
+        [block, from_high, jnp.concatenate([far_left, far_right], axis=1), from_low], axis=0
+    )
+    up, down = shift_second(n, 1), shift_second(n, -1)
+    line_low = lax.ppermute(line, "dp", up)
+    line_high = lax.ppermute(line, "dp", down)
+    line_far_left = lax.ppermute(line_low[:, :half], "dp", up)
+    line_far_right = lax.ppermute(line_high[:, half:], "dp", down)
+    mine = [line, line_high, (line_far_left, line_far_right), line_low]
+    swap = [(i, i ^ 1) for i in range(n)]
+    other = [
+        lax.ppermute(line, "dp", swap),
+        lax.ppermute(line_high, "dp", swap),
+        (lax.ppermute(line_far_left, "dp", swap), lax.ppermute(line_far_right, "dp", swap)),
+        lax.ppermute(line_low, "dp", swap),
+    ]
+    return mine + other
+
+
+def block_order(n):
+    table = np.zeros((n, n), np.int32)
+    for i in range(n):
+        x, y, c = coords(i)
+        out = []
+        for cc in (c, 1 - c):
+            for db in range(SIDE):
+                for da in range(SIDE):
+                    out.append(index_of(x + da, y + db, 0) if cc == 0 else index_of(x + db, y + da, 1))
+        table[i] = out
+    return table
 
 
 def body(out_grad, expert_ids, route_weights, pre_activations, down_weight):
@@ -14,14 +79,17 @@
     ndp = lax.axis_size("dp")
     rows = down_weight.shape[1]
     n_all = ndp * tok
+    half = width // 2
 
-    nex = lax.axis_size("expert")
-    w_all = lax.all_to_all(
-        jnp.broadcast_to(down_weight, (nex,) + down_weight.shape[1:]), "expert", 0, 0, tiled=True
-    )
+    w_all = lax.all_gather(down_weight, "expert", axis=0, tiled=True)
     experts = w_all.shape[0]
     wcat = w_all.reshape(experts * rows, width)
-    og_all = lax.all_gather(out_grad, "dp", axis=0, tiled=True)
+
+    pieces = ring_gather(out_grad, ndp)
+    table = block_order(ndp)
+    me = lax.axis_index("dp")
+    order = jnp.asarray(table)[me]
+    inverse = jnp.asarray(np.argsort(table, axis=1).astype(np.int32))[me]
 
     gate = pre_activations[..., :units].astype(F32)
     up = pre_activations[..., units:].astype(F32)
@@ -32,6 +100,7 @@
     meta = jnp.stack([expert_ids.T.astype(BF16), route_weights.T], axis=1)
     send_h = jnp.concatenate([send_h, jnp.broadcast_to(meta[None], (ndp, top, 2, tok))], axis=2)
     got_h = lax.all_to_all(send_h, "dp", 0, 0, tiled=True)
+    got_h = jnp.take(got_h, order, axis=0)
     got_h = got_h.transpose(1, 2, 0, 3).reshape(top, rows + 2, n_all)
     hid_t = got_h[:, :rows].astype(F32)
     ids_t = got_h[:, rows].astype(F32)
@@ -42,17 +111,46 @@
     for k in range(top):
         hp = hp + jnp.where(ids_t[k][None, None, :] == eidx, (rw_t[k][None, :] * hid_t[k])[None], 0.0)
     hp = hp.reshape(experts * rows, n_all).astype(BF16)
-    part = lax.dot_general(hp, og_all, (((1,), (0,)), ((), ())), preferred_element_type=F32)
+
+    def tn(a, b):
+        return lax.dot_general(a, b, (((1,), (0,)), ((), ())), preferred_element_type=F32)
+
+    def nt(a, b):
+        return lax.dot_general(a, b, (((1,), (1,)), ((), ())), preferred_element_type=F32)
+
+    part = jnp.zeros((experts * rows, width), F32)
+    part_left = jnp.zeros((experts * rows, half), F32)
+    part_right = jnp.zeros((experts * rows, half), F32)
+    start = 0
+    for piece in pieces:
+        if isinstance(piece, tuple):
+            left, right = piece
+            count = left.shape[0]
+            cols = hp[:, start : start + count]
+            part_left = part_left + tn(cols, left)
+            part_right = part_right + tn(cols, right)
+        else:
+            count = piece.shape[0]
+            part = part + tn(hp[:, start : start + count], piece)
+        start += count
+    part = part + jnp.concatenate([part_left, part_right], axis=1)
     part = part.reshape(experts, rows, width).astype(BF16)
     part, wcat = lax.optimization_barrier((part, wcat))
 
-    r_t = lax.dot_general(wcat, og_all, (((1,), (1,)), ((), ())), preferred_element_type=F32)
-    r_t = r_t.reshape(experts, rows, n_all)
+    r_list = []
+    for piece in pieces:
+        if isinstance(piece, tuple):
+            left, right = piece
+            r_list.append(nt(wcat[:, :half], left) + nt(wcat[:, half:], right))
+        else:
+            r_list.append(nt(wcat, piece))
+    r_t = jnp.concatenate(r_list, axis=1).reshape(experts, rows, n_all)
     hg_t = jnp.stack(
         [jnp.sum(jnp.where(ids_t[k][None, None, :] == eidx, r_t, 0.0), axis=0) for k in range(top)]
     ).astype(BF16)
 
     send_g = hg_t.reshape(top, rows, ndp, tok).transpose(2, 0, 1, 3)
+    send_g = jnp.take(send_g, inverse, axis=0)
     got_g = lax.all_to_all(send_g, "dp", 0, 0, tiled=True)
     hidden_grad = got_g.transpose(3, 1, 0, 2).reshape(tok, top, units)
 

time: 199 us -> 204 us (1.025)
  waiting for transfers between devices: 92.6 us -> 59.8 us
  starting transfers between devices: 22.3 us -> 54.6 us
  blocking collectives: 21.5 us -> 0 us
  other arithmetic: 12 us -> 22.7 us
  matrix products: 24.5 us -> 33.9 us
  local copies, waits for them, and re-layouts: 11.3 us -> 16.6 us
    all_gather x1, waiting for transfers between devices: 46.4 us -> 0.01 us  [body(): w_all = lax.all_gather(down_weight, 'expert', axis=0, tiled=True)]
    ppermute x0 -> x13, starting transfers between devices: none -> 38.8 us  [the longest x1 5.51 us: ring_gather(): line_far_left = lax.ppermute(line_low[:, :half], 'dp', up)]
    ppermute x0 -> x13, waiting for transfers between devices: none -> 24.1 us  [the longest x1 15.7 us: ring_gather(): line_low = lax.ppermute(line, 'dp', up)]
    all_to_all x1 -> x0, blocking collectives: 21.5 us -> none  [body(): got_h = lax.all_to_all(send_h, 'dp', 0, 0, tiled=True)]
    dot_general x2 -> x20, matrix products: 24.5 us -> 33.9 us  [the longest x10 17.7 us: nt(): lax.dot_general(a, b, (((1,), (1,)), ((), ())), preferred_element_type=F32)]
    reduce_scatter x1, waiting for transfers between devices: 28.6 us -> 22.6 us  [body(): summed = lax.psum_scatter(part, 'expert', scatter_dimension=0, tiled=True)]
    all_to_all x1, waiting for transfers between devices: 4.51 us -> 0.01 us  [body(): got_h = lax.all_to_all(send_h, 'dp', 0, 0, tiled=True)]
    all_to_all x1, starting transfers between devices: 14 us -> 9.82 us  [body(): got_h = lax.all_to_all(send_h, 'dp', 0, 0, tiled=True)]
  transfers between devices with their start and end apart: 4 -> 17, of which waited for: 4 -> 5; matrix products, arithmetic and copies ran while one was open for 23% -> 34% of each run, Pallas kernels for 0% -> 0%
where the time goes in v4:
time: 204 us; the launch traced here: 203 us
  waiting for transfers between devices  59.8 us (29%)
  starting transfers between devices  54.6 us (27%)
  matrix products  33.9 us (17%)
  other arithmetic  22.7 us (11%)
  local copies, waits for them, and re-layouts  16.6 us (8%)
  between operations  14.9 us (7%)
    reduce_scatter x1, waiting for transfers between devices, body(): summed = lax.psum_scatter(part, 'expert', scatter_dimension=0, tiled=True)  22.6 us
    dot_general x10, matrix products, nt(): lax.dot_general(a, b, (((1,), (1,)), ((), ())), preferred_element_type=F32)  17.7 us
    dot_general x10, matrix products, tn(): lax.dot_general(a, b, (((1,), (0,)), ((), ())), preferred_element_type=F32)  16.2 us
    ppermute x1, waiting for transfers between devices, ring_gather(): line_low = lax.ppermute(line, 'dp', up)  15.7 us
    all_to_all x1, waiting for transfers between devices, body(): got_g = lax.all_to_all(send_g, 'dp', 0, 0, tiled=True)  12.5 us
    all_to_all x1, starting transfers between devices, body(): got_h = lax.all_to_all(send_h, 'dp', 0, 0, tiled=True)  9.82 us
    unnamed x59, local copies, waits for them, and re-layouts  6.86 us
    all_to_all x1, starting transfers between devices, body(): got_g = lax.all_to_all(send_g, 'dp', 0, 0, tiled=True)  5.9 us
  transfers between devices with their start and end apart: 17, of which 5 were waited for; matrix products, arithmetic and copies ran while one was open for 34% of the time, Pallas kernels for 0%

profile of v4, /device:TPU:24, one launch (start us, length us, event | category | flops | bytes accessed | tf_op | source)
XLA Modules:
  0.0 202.6 jit_solution(2583801669065490339)
XLA Ops:
  7.2 3.4 %collective-permute-start.1 = (bf16[128,2048]{1,0:T(8,128)(2,1)}, bf16[128,2048]{1,0:T(8,128)(2,1)S(1)}, u32[]{:S(2)}, u32[]{:S(2)}) collective-permute-start(bf16[128,2048]{1,0:T(8,128)(2,1)} %param.7), channel_id=1, source_target_pairs={{0,128},{16,48},{32,160},{48,80},{64,192},{80,112},{96,224},{112,1... | collective-permute-start | bytes 1572872 | tf_op jit(solution)/shard_map/ppermute | solution.py:39
  10.6 3.7 %collective-permute-start = (bf16[128,2048]{1,0:T(8,128)(2,1)}, bf16[128,2048]{1,0:T(8,128)(2,1)S(1)}, u32[]{:S(2)}, u32[]{:S(2)}) collective-permute-start(bf16[128,2048]{1,0:T(8,128)(2,1)} %param.7), channel_id=1, source_target_pairs={{0,384},{16,112},{32,416},{48,16},{64,448},{80,48},{96,480},{112,8... | collective-permute-start | bytes 1572872 | tf_op jit(solution)/shard_map/ppermute | solution.py:40
  20.2 9.8 %all-to-all-start = ((bf16[32,4,26,128]{3,1,2,0:T(4,128)(2,1)}), bf16[32,4,26,128]{3,1,2,0:T(4,128)(2,1)}, u32[]{:S(2)}, u32[]{:S(2)}) async-start(bf16[32,4,26,128]{3,1,2,0:T(4,128)(2,1)} %pad_maximum_fusion.2), calls=%async_computation | async-start | bytes 1703936 | tf_op jit(solution)/shard_map/all_to_all | solution.py:102
  32.9 3.4 %collective-permute-start.2 = (bf16[128,1024]{1,0:T(8,128)(2,1)S(1)}, bf16[128,1024]{1,0:T(8,128)(2,1)S(1)}, u32[]{:S(2)}, u32[]{:S(2)}) collective-permute-start(bf16[128,1024]{1,0:T(8,128)(2,1)S(1)} %slice.158), channel_id=1, source_target_pairs={{0,128},{16,48},{32,160},{48,80},{64,192},{80,112},{96,224},{112,1... | collective-permute-start | bytes 786440 | tf_op jit(solution)/shard_map/ppermute | solution.py:41
  36.4 3.6 %collective-permute-start.3 = (bf16[128,1024]{1,0:T(8,128)(2,1)S(1)}, bf16[128,1024]{1,0:T(8,128)(2,1)S(1)}, u32[]{:S(2)}, u32[]{:S(2)}) collective-permute-start(bf16[128,1024]{1,0:T(8,128)(2,1)S(1)} %slice.159), channel_id=1, source_target_pairs={{0,384},{16,112},{32,416},{48,16},{64,448},{80,48},{96,480},{112,8... | collective-permute-start | bytes 786440 | tf_op jit(solution)/shard_map/ppermute | solution.py:42
  40.7 5.0 %collective-permute-done.2 = bf16[128,1024]{1,0:T(8,128)(2,1)S(1)} collective-permute-done((bf16[128,1024]{1,0:T(8,128)(2,1)S(1)}, bf16[128,1024]{1,0:T(8,128)(2,1)S(1)}, u32[]{:S(2)}, u32[]{:S(2)}) %collective-permute-start.2) | collective-permute-done | bytes 262176 | tf_op jit(solution)/shard_map/ppermute | solution.py:41
  45.8 3.0 %pad_maximum_fusion = bf16[512,2048]{1,0:T(8,128)(2,1)} fusion(bf16[128,2048]{1,0:T(8,128)(2,1)S(1)} %collective-permute-done.1, bf16[128,1024]{1,0:T(8,128)(2,1)S(1)} %collective-permute-done.3, bf16[128,1024]{1,0:T(8,128)(2,1)S(1)} %collective-permute-done.2, bf16[128,2048]{1,0:T(8,128)(2,1)S(1)} %collective-permute-done, bf16[128,2048]{1,0:T(8,128)(2,1)} %param.7), kind=kLoop, calls=%fused_computation.13 | loop fusion | flops 10485760 | bytes 4194304 | tf_op jit(solution)/shard_map/concatenate | solution.py:43
  48.8 2.7 %collective-permute-start.4 = (bf16[512,2048]{1,0:T(8,128)(2,1)}, bf16[512,2048]{1,0:T(8,128)(2,1)}, u32[]{:S(2)}, u32[]{:S(2)}) collective-permute-start(bf16[512,2048]{1,0:T(8,128)(2,1)} %pad_maximum_fusion), channel_id=1, source_target_pairs={{0,96},{16,400},{32,0},{48,432},{64,32},{80,464},{96,64},{112,496}... | collective-permute-start | bytes 6291464 | tf_op jit(solution)/shard_map/ppermute | solution.py:48
  51.5 4.3 %collective-permute-start.5 = (bf16[512,2048]{1,0:T(8,128)(2,1)}, bf16[512,2048]{1,0:T(8,128)(2,1)}, u32[]{:S(2)}, u32[]{:S(2)}) collective-permute-start(bf16[512,2048]{1,0:T(8,128)(2,1)} %pad_maximum_fusion), channel_id=1, source_target_pairs={{0,32},{16,144},{32,64},{48,176},{64,96},{80,208},{96,0},{112,240}... | collective-permute-start | bytes 6291464 | tf_op jit(solution)/shard_map/ppermute | solution.py:47
  64.1 15.7 %collective-permute-done.5 = bf16[512,2048]{1,0:T(8,128)(2,1)} collective-permute-done((bf16[512,2048]{1,0:T(8,128)(2,1)}, bf16[512,2048]{1,0:T(8,128)(2,1)}, u32[]{:S(2)}, u32[]{:S(2)}) %collective-permute-start.5) | collective-permute-done | bytes 2097184 | tf_op jit(solution)/shard_map/ppermute | solution.py:47
  81.1 5.5 %collective-permute-start.9 = (bf16[512,1024]{1,0:T(8,128)(2,1)S(1)}, bf16[512,1024]{1,0:T(8,128)(2,1)S(1)}, u32[]{:S(2)}, u32[]{:S(2)}) collective-permute-start(bf16[512,1024]{1,0:T(8,128)(2,1)S(1)} %slice.166), channel_id=1, source_target_pairs={{0,32},{16,144},{32,64},{48,176},{64,96},{80,208},{96,0},{112,240}... | collective-permute-start | bytes 3145736 | tf_op jit(solution)/shard_map/ppermute | solution.py:49
  86.6 3.0 %add_convert_fusion = bf16[16,24,4096]{2,1,0:T(8,128)(2,1)S(1)} fusion(f32[24,4096]{1,0:T(8,128)S(1)} %bitcast.124, f32[24,4096]{1,0:T(8,128)S(1)} %bitcast.125, f32[24,4096]{1,0:T(8,128)S(1)} %bitcast.126, f32[24,4096]{1,0:T(8,128)S(1)} %bitcast.127, pred[16,4096]{1,0:T(8,128)(4,1)S(1)} %iota_compare_fusion, pred[16,4096]{1,0:T(8,128)(4,1)S(1)} %iota_compare_fusion.1, ...), kind=kLoop, calls=%fused_computation.6 | loop fusion | flops 12582912 | bytes 4980736 | tf_op jit(solution)/shard_map/convert.12
  96.2 2.6 %fusion.28 = f32[384,2048]{1,0:T(8,128)S(1)} fusion(bf16[512,2048]{1,0:T(8,128)(2,1)} %collective-permute-done.5, bf16[384,4096]{1,0:T(8,128)(2,1)S(1)} %bitcast.111), kind=kOutput, calls=%fused_computation.62 | convolution fusion | flops 805306368 | bytes 5636096 | tf_op jit(solution)/shard_map/dot_general | solution.py:116
  105.7 3.3 %collective-permute-done.11 = bf16[512,1024]{1,0:T(8,128)(2,1)S(1)} collective-permute-done((bf16[512,1024]{1,0:T(8,128)(2,1)S(1)}, bf16[512,1024]{1,0:T(8,128)(2,1)S(1)}, u32[]{:S(2)}, u32[]{:S(2)}) %collective-permute-start.11) | collective-permute-done | bytes 1048608 | tf_op jit(solution)/shard_map/ppermute | solution.py:50
  118.0 4.2 %fusion = bf16[384,2048]{1,0:T(8,128)(2,1)} fusion(f32[384,1024]{1,0:T(8,128)S(1)} %convolution_add_fusion, f32[384,1024]{1,0:T(8,128)S(1)} %convolution_add_fusion.1, f32[384,2048]{1,0:T(8,128)S(1)} %fusion.24, f32[384,2048]{1,0:T(8,128)S(1)} %fusion.26, f32[384,2048]{1,0:T(8,128)S(1)} %fusion.28, f32[384,2048]{1,0:T(8,128)S(1)} %fusion.32, ...), kind=kOutput, calls=%fused_computation.8 | convolution fusion | flops 811597824 | bytes 22937600 | tf_op jit(solution)/shard_map/dot_general | solution.py:116
  122.3 3.1 %convolution_dynamic-update-slice_fusion.5 = f32[384,4096]{1,0:T(8,128)S(1)} fusion(bf16[384,2048]{1,0:T(8,128)(2,1)} %bitcast.128, bf16[128,2048]{1,0:T(8,128)(2,1)} %copy-done.5, bf16[128,1024]{1,0:T(8,128)(2,1)} %copy-done.20, bf16[128,1024]{1,0:T(8,128)(2,1)} %copy-done.18, bf16[128,2048]{1,0:T(8,128)(2,1)} %copy-done.7, bf16[128,2048]{1,0:T(8,128)(2,1)} %param.7), kind=kOutput, calls=%fused_computation.38 | convolution fusion | flops 815792128 | bytes 4456448 | tf_op jit(solution)/shard_map/dot_general | solution.py:119
  127.3 2.7 %convolution_dynamic-update-slice_fusion.4 = f32[384,4096]{1,0:T(8,128)S(1)} fusion(f32[384,4096]{1,0:T(8,128)S(1)} %convolution_dynamic-update-slice_fusion.5, bf16[384,2048]{1,0:T(8,128)(2,1)S(1)} %bitcast.131, bf16[512,2048]{1,0:T(8,128)(2,1)} %collective-permute-done.4), kind=kOutput, calls=%fused_computation.37 | convolution fusion | flops 805306368 | bytes 4456448 | tf_op jit(solution)/shard_map/dot_general | solution.py:119
  130.7 2.7 %convolution_dynamic-update-slice_fusion.3 = f32[384,4096]{1,0:T(8,128)S(1)} fusion(f32[384,4096]{1,0:T(8,128)S(1)} %fusion.13, bf16[384,2048]{1,0:T(8,128)(2,1)S(1)} %bitcast.133, bf16[512,2048]{1,0:T(8,128)(2,1)} %collective-permute-done.5), kind=kOutput, calls=%fused_computation.36 | convolution fusion | flops 805306368 | bytes 4456448 | tf_op jit(solution)/shard_map/dot_general | solution.py:119
  133.4 2.8 %convolution_dynamic-update-slice_fusion.2 = f32[384,4096]{1,0:T(8,128)S(1)} fusion(f32[384,4096]{1,0:T(8,128)S(1)} %convolution_dynamic-update-slice_fusion.3, bf16[384,2048]{1,0:T(8,128)(2,1)S(1)} %bitcast.134, bf16[512,2048]{1,0:T(8,128)(2,1)} %collective-permute-done.6), kind=kOutput, calls=%fused_computation.35 | convolution fusion | flops 805306368 | bytes 4456448 | tf_op jit(solution)/shard_map/dot_general | solution.py:119
  138.2 2.7 %convolution_dynamic-update-slice_fusion = f32[384,4096]{1,0:T(8,128)S(1)} fusion(f32[384,4096]{1,0:T(8,128)S(1)} %fusion.12, bf16[384,2048]{1,0:T(8,128)(2,1)S(1)} %bitcast.137, bf16[512,2048]{1,0:T(8,128)(2,1)} %collective-permute-done.8), kind=kOutput, calls=%fused_computation.33 | convolution fusion | flops 805306368 | bytes 4456448 | tf_op jit(solution)/shard_map/dot_general | solution.py:119
  140.9 3.6 %select_reduce_fusion.3 = (bf16[24,4096]{1,0:T(8,128)(2,1)S(1)}, bf16[24,4096]{1,0:T(8,128)(2,1)S(1)}, bf16[24,4096]{1,0:T(8,128)(2,1)S(1)}, bf16[24,4096]{1,0:T(8,128)(2,1)S(1)}) fusion(f32[16,24,4096]{2,1,0:T(8,128)S(1)} %bitcast.121, pred[16,4096]{1,0:T(8,128)(4,1)S(1)} %copy-done.16, pred[16,4096]{1,0:T(8,128)(4,1)S(1)} %iota_compare_fusion, ...), kind=kLoop, calls=%fused_computation.5 | loop fusion | flops 12189696 | bytes 7340032 | tf_op jit(solution)/shard_map/reduce_sum | solution.py:149
  148.8 5.9 %all-to-all-start.1 = ((bf16[32,4,24,128]{3,2,1,0:T(8,128)(2,1)}), bf16[32,4,24,128]{3,2,1,0:T(8,128)(2,1)S(1)}, u32[]{:S(2)}, u32[]{:S(2)}) async-start(bf16[32,4,24,128]{3,2,1,0:T(8,128)(2,1)} %broadcast_select_fusion), calls=%async_computation.1 | async-start | bytes 1572864 | tf_op jit(solution)/shard_map/all_to_all | solution.py:154
  154.7 12.5 %all-to-all-done.1 = bf16[32,4,24,128]{3,2,1,0:T(8,128)(2,1)S(1)} async-done(((bf16[32,4,24,128]{3,2,1,0:T(8,128)(2,1)}), bf16[32,4,24,128]{3,2,1,0:T(8,128)(2,1)S(1)}, u32[]{:S(2)}, u32[]{:S(2)}) %all-to-all-start.1) | async-done | bytes 786464 | tf_op jit(solution)/shard_map/all_to_all | solution.py:154
  171.7 22.6 %reduce-scatter.2.cloned.1.call-done = bf16[1,24,2048]{2,1,0:T(8,128)(2,1)} async-done(((bf16[16,24,2048]{2,1,0:T(8,128)(2,1)}), bf16[1,24,2048]{2,1,0:T(8,128)(2,1)}) %reduce-scatter.2.cloned.1.call-update) | async-done | bytes 98320 | tf_op jit(solution)/shard_map/reduce_scatter | solution.py:164
  (134 shorter events, 55.7 us)
Async XLA Ops:
  7.2 25.7 %collective-permute-start.1 = (bf16[128,2048]{1,0:T(8,128)(2,1)}, bf16[128,2048]{1,0:T(8,128)(2,1)S(1)}, u32[]{:S(2)}, u32[]{:S(2)}) collective-permute-start(bf16[128,2048]{1,0:T(8,128)(2,1)} %param.7), channel_id=1, source_target_pairs={{0,128},{16,48},{32,160},{48,80},{64,192},{80,112},{96,224},{112,1... | collective-permute-start | bytes 1572872 | tf_op jit(solution)/shard_map/ppermute | solution.py:39
  10.6 25.8 %collective-permute-start = (bf16[128,2048]{1,0:T(8,128)(2,1)}, bf16[128,2048]{1,0:T(8,128)(2,1)S(1)}, u32[]{:S(2)}, u32[]{:S(2)}) collective-permute-start(bf16[128,2048]{1,0:T(8,128)(2,1)} %param.7), channel_id=1, source_target_pairs={{0,384},{16,112},{32,416},{48,16},{64,448},{80,48},{96,480},{112,8... | collective-permute-start | bytes 1572872 | tf_op jit(solution)/shard_map/ppermute | solution.py:40
  20.2 37.7 %all-to-all-start = ((bf16[32,4,26,128]{3,1,2,0:T(4,128)(2,1)}), bf16[32,4,26,128]{3,1,2,0:T(4,128)(2,1)}, u32[]{:S(2)}, u32[]{:S(2)}) async-start(bf16[32,4,26,128]{3,1,2,0:T(4,128)(2,1)} %pad_maximum_fusion.2), calls=%async_computation | async-start | bytes 1703936 | tf_op jit(solution)/shard_map/all_to_all | solution.py:102
  30.0 92.3 %all-gather.2.cloned.1.call-start = ((), (), s32[]{:S(2)}) async-start(), calls=%async_computation.3 | async-start | bytes 1671168 | tf_op jit(solution)/shard_map/all_gather | solution.py:84
  30.7 163.5 %reduce-scatter.2.cloned.1.call-start = ((), (), s32[]{:S(2)}) async-start(), calls=%async_computation.4 | async-start | bytes 1671168 | tf_op jit(solution)/shard_map/reduce_scatter | solution.py:164
  32.9 24.9 %copy-start.5 = (bf16[128,2048]{1,0:T(8,128)(2,1)}, bf16[128,2048]{1,0:T(8,128)(2,1)S(1)}, u32[]{:S(2)}) copy-start(bf16[128,2048]{1,0:T(8,128)(2,1)S(1)} %collective-permute-done.1) | copy-start | bytes 1572868
  32.9 12.9 %collective-permute-start.2 = (bf16[128,1024]{1,0:T(8,128)(2,1)S(1)}, bf16[128,1024]{1,0:T(8,128)(2,1)S(1)}, u32[]{:S(2)}, u32[]{:S(2)}) collective-permute-start(bf16[128,1024]{1,0:T(8,128)(2,1)S(1)} %slice.158), channel_id=1, source_target_pairs={{0,128},{16,48},{32,160},{48,80},{64,192},{80,112},{96,224},{112,1... | collective-permute-start | bytes 786440 | tf_op jit(solution)/shard_map/ppermute | solution.py:41
  36.3 12.5 %copy-start.7 = (bf16[128,2048]{1,0:T(8,128)(2,1)}, bf16[128,2048]{1,0:T(8,128)(2,1)S(1)}, u32[]{:S(2)}) copy-start(bf16[128,2048]{1,0:T(8,128)(2,1)S(1)} %collective-permute-done) | copy-start | bytes 1572868
  36.4 9.4 %collective-permute-start.3 = (bf16[128,1024]{1,0:T(8,128)(2,1)S(1)}, bf16[128,1024]{1,0:T(8,128)(2,1)S(1)}, u32[]{:S(2)}, u32[]{:S(2)}) collective-permute-start(bf16[128,1024]{1,0:T(8,128)(2,1)S(1)} %slice.159), channel_id=1, source_target_pairs={{0,384},{16,112},{32,416},{48,16},{64,448},{80,48},{96,480},{112,8... | collective-permute-start | bytes 786440 | tf_op jit(solution)/shard_map/ppermute | solution.py:42
  45.8 5.8 %copy-start.18 = (bf16[128,1024]{1,0:T(8,128)(2,1)}, bf16[128,1024]{1,0:T(8,128)(2,1)S(1)}, u32[]{:S(2)}) copy-start(bf16[128,1024]{1,0:T(8,128)(2,1)S(1)} %collective-permute-done.2) | copy-start | bytes 786436
  45.8 10.1 %copy-start.20 = (bf16[128,1024]{1,0:T(8,128)(2,1)}, bf16[128,1024]{1,0:T(8,128)(2,1)S(1)}, u32[]{:S(2)}) copy-start(bf16[128,1024]{1,0:T(8,128)(2,1)S(1)} %collective-permute-done.3) | copy-start | bytes 786436
  48.8 40.9 %collective-permute-start.4 = (bf16[512,2048]{1,0:T(8,128)(2,1)}, bf16[512,2048]{1,0:T(8,128)(2,1)}, u32[]{:S(2)}, u32[]{:S(2)}) collective-permute-start(bf16[512,2048]{1,0:T(8,128)(2,1)} %pad_maximum_fusion), channel_id=1, source_target_pairs={{0,96},{16,400},{32,0},{48,432},{64,32},{80,464},{96,64},{112,496}... | collective-permute-start | bytes 6291464 | tf_op jit(solution)/shard_map/ppermute | solution.py:48
  51.5 28.2 %collective-permute-start.5 = (bf16[512,2048]{1,0:T(8,128)(2,1)}, bf16[512,2048]{1,0:T(8,128)(2,1)}, u32[]{:S(2)}, u32[]{:S(2)}) collective-permute-start(bf16[512,2048]{1,0:T(8,128)(2,1)} %pad_maximum_fusion), channel_id=1, source_target_pairs={{0,32},{16,144},{32,64},{48,176},{64,96},{80,208},{96,0},{112,240}... | collective-permute-start | bytes 6291464 | tf_op jit(solution)/shard_map/ppermute | solution.py:47
  55.9 55.1 %collective-permute-start.6 = (bf16[512,2048]{1,0:T(8,128)(2,1)}, bf16[512,2048]{1,0:T(8,128)(2,1)}, u32[]{:S(2)}, u32[]{:S(2)}) collective-permute-start(bf16[512,2048]{1,0:T(8,128)(2,1)} %pad_maximum_fusion), channel_id=1, source_target_pairs={{0,16},{16,0},{32,48},{48,32},{64,80},{80,64},{96,112},{112,96},{1... | collective-permute-start | bytes 6291464 | tf_op jit(solution)/shard_map/ppermute | solution.py:54
  63.0 23.6 %copy-start.13 = (pred[16,4096]{1,0:T(8,128)(4,1)}, pred[16,4096]{1,0:T(8,128)(4,1)S(1)}, u32[]{:S(2)}) copy-start(pred[16,4096]{1,0:T(8,128)(4,1)S(1)} %iota_compare_fusion.2) | copy-start | bytes 196612
  64.1 22.6 %copy-start.15 = (pred[16,4096]{1,0:T(8,128)(4,1)}, pred[16,4096]{1,0:T(8,128)(4,1)S(1)}, u32[]{:S(2)}) copy-start(pred[16,4096]{1,0:T(8,128)(4,1)S(1)} %iota_compare_fusion.3) | copy-start | bytes 196612
  81.1 20.1 %collective-permute-start.9 = (bf16[512,1024]{1,0:T(8,128)(2,1)S(1)}, bf16[512,1024]{1,0:T(8,128)(2,1)S(1)}, u32[]{:S(2)}, u32[]{:S(2)}) collective-permute-start(bf16[512,1024]{1,0:T(8,128)(2,1)S(1)} %slice.166), channel_id=1, source_target_pairs={{0,32},{16,144},{32,64},{48,176},{64,96},{80,208},{96,0},{112,240}... | collective-permute-start | bytes 3145736 | tf_op jit(solution)/shard_map/ppermute | solution.py:49
  91.1 17.9 %collective-permute-start.11 = (bf16[512,1024]{1,0:T(8,128)(2,1)S(1)}, bf16[512,1024]{1,0:T(8,128)(2,1)S(1)}, u32[]{:S(2)}, u32[]{:S(2)}) collective-permute-start(bf16[512,1024]{1,0:T(8,128)(2,1)S(1)} %slice.168), channel_id=1, source_target_pairs={{0,96},{16,400},{32,0},{48,432},{64,32},{80,464},{96,64},{112,496}... | collective-permute-start | bytes 3145736 | tf_op jit(solution)/shard_map/ppermute | solution.py:50
  94.1 22.6 %collective-permute-start.7 = (bf16[512,2048]{1,0:T(8,128)(2,1)}, bf16[512,2048]{1,0:T(8,128)(2,1)S(1)}, u32[]{:S(2)}, u32[]{:S(2)}) collective-permute-start(bf16[512,2048]{1,0:T(8,128)(2,1)} %collective-permute-done.4), channel_id=1, source_target_pairs={{0,16},{16,0},{32,48},{48,32},{64,80},{80,64},{96,112},{112,96},{1... | collective-permute-start | bytes 6291464 | tf_op jit(solution)/shard_map/ppermute | solution.py:55
  98.8 19.3 %collective-permute-start.8 = (bf16[512,2048]{1,0:T(8,128)(2,1)}, bf16[512,2048]{1,0:T(8,128)(2,1)}, u32[]{:S(2)}, u32[]{:S(2)}) collective-permute-start(bf16[512,2048]{1,0:T(8,128)(2,1)} %collective-permute-done.5), channel_id=1, source_target_pairs={{0,16},{16,0},{32,48},{48,32},{64,80},{80,64},{96,112},{112,96},{1... | collective-permute-start | bytes 6291464 | tf_op jit(solution)/shard_map/ppermute | solution.py:57
  101.2 13.5 %collective-permute-start.10 = (bf16[512,1024]{1,0:T(8,128)(2,1)S(1)}, bf16[512,1024]{1,0:T(8,128)(2,1)S(1)}, u32[]{:S(2)}, u32[]{:S(2)}) collective-permute-start(bf16[512,1024]{1,0:T(8,128)(2,1)S(1)} %collective-permute-done.9), channel_id=1, source_target_pairs={{0,16},{16,0},{32,48},{48,32},{64,80},{80,64},{96,112},{112,96},{1... | collective-permute-start | bytes 3145736 | tf_op jit(solution)/shard_map/ppermute | solution.py:56
  109.0 5.1 %copy-start.9 = (bf16[512,1024]{1,0:T(8,128)(2,1)}, bf16[512,1024]{1,0:T(8,128)(2,1)S(1)}, u32[]{:S(2)}) copy-start(bf16[512,1024]{1,0:T(8,128)(2,1)S(1)} %collective-permute-done.11) | copy-start | bytes 3145732
  109.0 6.7 %collective-permute-start.12 = (bf16[512,1024]{1,0:T(8,128)(2,1)S(1)}, bf16[512,1024]{1,0:T(8,128)(2,1)S(1)}, u32[]{:S(2)}, u32[]{:S(2)}) collective-permute-start(bf16[512,1024]{1,0:T(8,128)(2,1)S(1)} %collective-permute-done.11), channel_id=1, source_target_pairs={{0,16},{16,0},{32,48},{48,32},{64,80},{80,64},{96,112},{112,96},{1... | collective-permute-start | bytes 3145736 | tf_op jit(solution)/shard_map/ppermute | solution.py:56
  148.8 18.4 %all-to-all-start.1 = ((bf16[32,4,24,128]{3,2,1,0:T(8,128)(2,1)}), bf16[32,4,24,128]{3,2,1,0:T(8,128)(2,1)S(1)}, u32[]{:S(2)}, u32[]{:S(2)}) async-start(bf16[32,4,24,128]{3,2,1,0:T(8,128)(2,1)} %broadcast_select_fusion), calls=%async_computation.1 | async-start | bytes 1572864 | tf_op jit(solution)/shard_map/all_to_all | solution.py:154
  (17 other events, 40.3 us)
Sparse Core Ops, SparseCore 0:
  32.9 72.2 all-gather.1
  122.4 71.7 reduce-scatter.1

commit v5 on v2

v5 whole, which is shorter than its diff:
```python
import jax
import numpy as np
import jax.numpy as jnp
from jax import lax
from jax.sharding import Mesh, PartitionSpec as P

PLANE = ("mx", "my", "mc")

F32 = jnp.float32
BF16 = jnp.bfloat16


def body(out_grad, expert_ids, route_weights, pre_activations, down_weight):
    tok, width = out_grad.shape
    top = expert_ids.shape[1]
    units = pre_activations.shape[2] // 2
    ndp = lax.axis_size(PLANE)
    rows = down_weight.shape[1]
    n_all = ndp * tok

    nex = lax.axis_size("expert")
    w_all = lax.all_to_all(
        jnp.broadcast_to(down_weight, (nex,) + down_weight.shape[1:]), "expert", 0, 0, tiled=True
    )
    experts = w_all.shape[0]
    wcat = w_all.reshape(experts * rows, width)
    core = lax.axis_index("mc")
    og_mine = lax.all_gather(out_grad, ("mx", "my"), axis=0, tiled=True)
    og_other = lax.ppermute(og_mine, "mc", [(0, 1), (1, 0)])
    nhalf = og_mine.shape[0]
    table = np.stack([np.concatenate([np.arange(ndp // 2) * 2 + c, np.arange(ndp // 2) * 2 + 1 - c]) for c in (0, 1)])
    order = jnp.asarray(table.astype(np.int32))[core]
    inverse = jnp.asarray(np.argsort(table, axis=1).astype(np.int32))[core]

    gate = pre_activations[..., :units].astype(F32)
    up = pre_activations[..., units:].astype(F32)
    sig = jax.nn.sigmoid(gate)
    hidden = (gate * sig * up).astype(BF16)

    send_h = hidden.reshape(tok, top, ndp, rows).transpose(2, 1, 3, 0)
    meta = jnp.stack([expert_ids.T.astype(BF16), route_weights.T], axis=1)
    send_h = jnp.concatenate([send_h, jnp.broadcast_to(meta[None], (ndp, top, 2, tok))], axis=2)
    got_h = lax.all_to_all(send_h, PLANE, 0, 0, tiled=True)
    got_h = jnp.take(got_h, order, axis=0)
    got_h = got_h.transpose(1, 2, 0, 3).reshape(top, rows + 2, n_all)
    hid_t = got_h[:, :rows].astype(F32)
    ids_t = got_h[:, rows].astype(F32)
    rw_t = got_h[:, rows + 1].astype(F32)

    eidx = jnp.arange(experts, dtype=F32)[:, None, None]
    hp = jnp.zeros((experts, rows, n_all), F32)
    for k in range(top):
        hp = hp + jnp.where(ids_t[k][None, None, :] == eidx, (rw_t[k][None, :] * hid_t[k])[None], 0.0)
    hp = hp.reshape(experts * rows, n_all).astype(BF16)
    part = lax.dot_general(hp[:, :nhalf], og_mine, (((1,), (0,)), ((), ())), preferred_element_type=F32)
    part = part + lax.dot_general(hp[:, nhalf:], og_other, (((1,), (0,)), ((), ())), preferred_element_type=F32)
    part = part.reshape(experts, rows, width).astype(BF16)
    part, wcat = lax.optimization_barrier((part, wcat))

    r_t = jnp.concatenate(
        [lax.dot_general(wcat, og, (((1,), (1,)), ((), ())), preferred_element_type=F32) for og in (og_mine, og_other)],
        axis=1,
    )
    r_t = r_t.reshape(experts, rows, n_all)
    hg_t = jnp.stack(
        [jnp.sum(jnp.where(ids_t[k][None, None, :] == eidx, r_t, 0.0), axis=0) for k in range(top)]
    ).astype(BF16)

    send_g = hg_t.reshape(top, rows, ndp, tok).transpose(2, 0, 1, 3)
    send_g = jnp.take(send_g, inverse, axis=0)
    got_g = lax.all_to_all(send_g, PLANE, 0, 0, tiled=True)
    hidden_grad = got_g.transpose(3, 1, 0, 2).reshape(tok, top, units)

    hg32 = hidden_grad.astype(F32)
    weight_grad = jnp.sum(hg32 * hidden.astype(F32), axis=-1).astype(BF16)
    cot = route_weights.astype(F32)[..., None] * hg32
    gate_grad = cot * up * sig * (1.0 + gate * (1.0 - sig))
    up_grad = cot * gate * sig
    pre_grad = jnp.concatenate([gate_grad, up_grad], axis=-1).astype(BF16)

    summed = lax.psum_scatter(part, "expert", scatter_dimension=0, tiled=True)
    down_grad = (summed.astype(F32) / ndp).astype(BF16)
    return pre_grad, weight_grad, down_grad


def solution(mesh):
    side = 4
    plane = Mesh(
        mesh.devices.reshape(side, mesh.devices.shape[0] // (2 * side), 2, mesh.devices.shape[1]),
        PLANE + ("expert",),
    )
    tokens = (PLANE + ("expert",),)
    return jax.shard_map(
        body,
        mesh=plane,
        in_specs=(
            P(tokens[0], None),
            P(tokens[0], None),
            P(tokens[0], None),
            P(tokens[0], None, None),
            P("expert", PLANE, None),
        ),
        out_specs=(
            P(tokens[0], None, None),
            P(tokens[0], None),
            P("expert", PLANE, None),
        ),
        check_vma=False,
    )
```

time: 199 us -> 206 us (1.035)
  blocking collectives: 21.5 us -> 0 us
  waiting for transfers between devices: 92.6 us -> 104 us
  other arithmetic: 12 us -> 20.7 us
  starting transfers between devices: 22.3 us -> 30.2 us
  local copies, waits for them, and re-layouts: 11.3 us -> 16.6 us
  matrix products: 24.5 us -> 19.4 us
    all_to_all x1 -> x0, blocking collectives: 21.5 us -> none  [body(): got_h = lax.all_to_all(send_h, 'dp', 0, 0, tiled=True)]
    all_to_all x1 -> x2, waiting for transfers between devices: 12.5 us -> 25.6 us  [the longest x1 13.1 us: body(): got_h = lax.all_to_all(send_h, PLANE, 0, 0, tiled=True)]
    all_to_all x1 -> x2, starting transfers between devices: 8.21 us -> 14.4 us  [the longest x1 9.17 us: body(): got_h = lax.all_to_all(send_h, PLANE, 0, 0, tiled=True)]
    dot_general x2 -> x4, matrix products: 24.5 us -> 19.4 us  [the longest x2 11.4 us: body(): lax.dot_general(wcat, og, (((1,), (1,)), ((), ())), preferred_element_typ...]
    gather x0 -> x2, local copies, waits for them, and re-layouts: none -> 3.96 us  [the longest x1 2.43 us: body(): got_h = jnp.take(got_h, order, axis=0)]
    another operation x1 -> x2, other arithmetic: 1.63 us -> 4.75 us
    all_to_all x1, waiting for transfers between devices: 4.51 us -> 1.72 us  [body(): lax.all_to_all(jnp.broadcast_to(down_weight, (nex,) + down_weight.shape[1...]
    unnamed x25 -> x29, local copies, waits for them, and re-layouts: 5.62 us -> 8.13 us
  transfers between devices with their start and end apart: 4 -> 6, of which waited for: 4 -> 6; matrix products, arithmetic and copies ran while one was open for 23% -> 25% of each run, Pallas kernels for 0% -> 0%
where the time goes in v5:
time: 206 us; the launch traced here: 205 us
  waiting for transfers between devices  104 us (50%)
  starting transfers between devices  30.2 us (15%)
  other arithmetic  20.7 us (10%)
  matrix products  19.4 us (9%)
  local copies, waits for them, and re-layouts  16.6 us (8%)
  between operations  14.5 us (7%)
    all_gather x1, waiting for transfers between devices, body(): og_mine = lax.all_gather(out_grad, ('mx', 'my'), axis=0, tiled=True)  45.7 us
    reduce_scatter x1, waiting for transfers between devices, body(): summed = lax.psum_scatter(part, 'expert', scatter_dimension=0, tiled=True)  28.8 us
    all_to_all x1, starting transfers between devices, body(): lax.all_to_all(jnp.broadcast_to(down_weight, (nex,) + down_weight.shape[1...  13.8 us
    all_to_all x1, waiting for transfers between devices, body(): got_h = lax.all_to_all(send_h, PLANE, 0, 0, tiled=True)  13.1 us
    all_to_all x1, waiting for transfers between devices, body(): got_g = lax.all_to_all(send_g, PLANE, 0, 0, tiled=True)  12.5 us
    dot_general x2, matrix products, body(): lax.dot_general(wcat, og, (((1,), (1,)), ((), ())), preferred_element_typ...  11.4 us
    all_to_all x1, starting transfers between devices, body(): got_h = lax.all_to_all(send_h, PLANE, 0, 0, tiled=True)  9.17 us
    unnamed x29, local copies, waits for them, and re-layouts  8.13 us
  transfers between devices with their start and end apart: 6, of which 6 were waited for; matrix products, arithmetic and copies ran while one was open for 25% of the time, Pallas kernels for 0%

profile of v5, /device:TPU:24, one launch (start us, length us, event | category | flops | bytes accessed | tf_op | source)
XLA Modules:
  0.0 205.4 jit_solution(2487995461085984287)
XLA Ops:
  7.9 1.9 fusion.16
  13.9 9.2 %all-to-all-start = ((bf16[32,4,26,128]{3,1,2,0:T(4,128)(2,1)}), bf16[32,4,26,128]{3,1,2,0:T(4,128)(2,1)S(1)}, u32[]{:S(2)}, u32[]{:S(2)}) async-start(bf16[32,4,26,128]{3,1,2,0:T(4,128)(2,1)} %pad_maximum_fusion.2), calls=%async_computation | async-start | bytes 1703936 | tf_op jit(solution)/shard_map/all_to_all | solution.py:43
  23.2 13.1 %all-to-all-done = bf16[32,4,26,128]{3,1,2,0:T(4,128)(2,1)S(1)} async-done(((bf16[32,4,26,128]{3,1,2,0:T(4,128)(2,1)}), bf16[32,4,26,128]{3,1,2,0:T(4,128)(2,1)S(1)}, u32[]{:S(2)}, u32[]{:S(2)}) %all-to-all-start) | async-done | bytes 852000 | tf_op jit(solution)/shard_map/all_to_all | solution.py:43
  37.7 13.8 %all-to-all-start.1 = ((bf16[16,24,2048]{2,1,0:T(8,128)(2,1)}), bf16[16,24,2048]{2,1,0:T(8,128)(2,1)}, u32[]{:S(2)}, u32[]{:S(2)}) async-start(bf16[16,24,2048]{2,1,0:T(8,128)(2,1)} %broadcast_in_dim.138), calls=%async_computation.1 | async-start | bytes 3145728 | tf_op jit(solution)/shard_map/all_to_all | solution.py:22
  51.6 2.4 %gather_fusion = bf16[32,4,26,128]{3,1,2,0:T(4,128)(2,1)S(1)} fusion(bf16[32,4,26,128]{3,1,2,0:T(4,128)(2,1)} %copy-done, s32[1024]{0:T(1024)S(1)} %pad_clamp_fusion.1), kind=kCustom, calls=%fused_computation | custom fusion | bytes 1704064 | tf_op jit(solution)/shard_map/jit(_take)/gather | solution.py:44
  54.0 1.5 copy_bitcast_fusion
  55.6 45.7 %all-gather.2.cloned.1.call-done = bf16[2048,2048]{1,0:T(8,128)(2,1)} async-done(((bf16[128,2048]{1,0:T(8,128)(2,1)}), bf16[2048,2048]{1,0:T(8,128)(2,1)}) %all-gather.2.cloned.1.call-update) | async-done | bytes 8388624 | tf_op jit(solution)/shard_map/all_gather | solution.py:28
  101.3 1.9 collective-permute-start
  105.4 1.8 slice_multiply_fusion.3
  108.3 3.2 %add_convert_fusion = bf16[16,24,4096]{2,1,0:T(8,128)(2,1)S(1)} fusion(f32[24,4096]{1,0:T(8,128)S(1)} %bitcast.99, f32[24,4096]{1,0:T(8,128)S(1)} %bitcast.100, f32[24,4096]{1,0:T(8,128)S(1)} %bitcast.101, f32[24,4096]{1,0:T(8,128)S(1)} %bitcast.102, pred[16,4096]{1,0:T(8,128)(4,1)S(1)} %iota_compare_fusion, pred[16,4096]{1,0:T(8,128)(4,1)S(1)} %iota_compare_fusion.1, ...), kind=kLoop, calls=%fused_computation.7 | loop fusion | flops 12582912 | bytes 4980736 | tf_op jit(solution)/shard_map/convert.12
  111.5 3.5 %fusion.11 = f32[384,2048]{1,0:T(8,128)S(1)} fusion(bf16[2048,2048]{1,0:T(8,128)(2,1)S(1)} %copy-done.4, bf16[384,4096]{1,0:T(8,128)(2,1)S(1)} %bitcast.95), kind=kOutput, calls=%fused_computation.26 | convolution fusion | flops 3221225472 | bytes 13107200 | tf_op jit(solution)/shard_map/dot_general | solution.py:55
  116.5 3.2 %copy-done.5 = bf16[2048,2048]{1,0:T(8,128)(2,1)} copy-done((bf16[2048,2048]{1,0:T(8,128)(2,1)}, bf16[2048,2048]{1,0:T(8,128)(2,1)S(1)}, u32[]{:S(2)}) %copy-start.5) | copy-done | bytes 8388632
  119.8 4.6 %add_convert_fusion.1 = bf16[384,2048]{1,0:T(8,128)(2,1)} fusion(f32[384,2048]{1,0:T(8,128)S(1)} %fusion.11, bf16[2048,2048]{1,0:T(8,128)(2,1)S(1)} %collective-permute-done, bf16[384,4096]{1,0:T(8,128)(2,1)S(1)} %bitcast.96), kind=kOutput, calls=%fused_computation.8 | convolution fusion | flops 3222798336 | bytes 14680064 | tf_op jit(solution)/shard_map/dot_general | solution.py:56
  124.3 1.7 all-to-all-done.1
  126.1 6.5 %fusion.19 = f32[384,2048]{1,0:T(8,128)S(1)} fusion(bf16[384,2048]{1,0:T(8,128)(2,1)} %bitcast.22, bf16[2048,2048]{1,0:T(8,128)(2,1)} %all-gather.2.cloned.1.call-done), kind=kOutput, calls=%fused_computation.76 | convolution fusion | flops 3221225472 | bytes 13107200 | tf_op jit(solution)/shard_map/dot_general | solution.py:61
  132.6 4.8 %fusion.20 = f32[384,2048]{1,0:T(8,128)S(1)} fusion(bf16[384,2048]{1,0:T(8,128)(2,1)} %bitcast.22, bf16[2048,2048]{1,0:T(8,128)(2,1)S(1)} %copy-done.6), kind=kOutput, calls=%fused_computation.77 | convolution fusion | flops 3221225472 | bytes 13107200 | tf_op jit(solution)/shard_map/dot_general | solution.py:61
  138.1 3.6 %select_reduce_fusion.3 = (bf16[24,4096]{1,0:T(8,128)(2,1)S(1)}, bf16[24,4096]{1,0:T(8,128)(2,1)S(1)}, bf16[24,4096]{1,0:T(8,128)(2,1)S(1)}, bf16[24,4096]{1,0:T(8,128)(2,1)S(1)}) fusion(f32[16,24,4096]{2,1,0:T(8,128)S(1)} %bitcast.93, pred[16,4096]{1,0:T(8,128)(4,1)S(1)} %iota_compare_fusion.3, pred[16,4096]{1,0:T(8,128)(4,1)S(1)} %iota_compare_fusion, ...), kind=kLoop, calls=%fused_computation.6 | loop fusion | flops 12189696 | bytes 7340032 | tf_op jit(solution)/shard_map/reduce_sum | solution.py:66
  143.9 2.2 %broadcast_select_fusion = bf16[32,4,24,128]{3,2,1,0:T(8,128)(2,1)} fusion(bf16[32,4,24,128]{3,2,1,0:T(8,128)(2,1)} %gather_fusion.1, pred[32]{0:T(512)(128)(4,1)S(1)} %compare_and_fusion.1), kind=kLoop, calls=%fused_computation.39 | loop fusion | flops 393216 | bytes 1572896 | tf_op jit(solution)/shard_map/jit(_take)/select_n | solution.py:70
  146.0 5.2 %all-to-all-start.2 = ((bf16[32,4,24,128]{3,2,1,0:T(8,128)(2,1)}), bf16[32,4,24,128]{3,2,1,0:T(8,128)(2,1)S(1)}, u32[]{:S(2)}, u32[]{:S(2)}) async-start(bf16[32,4,24,128]{3,2,1,0:T(8,128)(2,1)} %broadcast_select_fusion), calls=%async_computation.2 | async-start | bytes 1572864 | tf_op jit(solution)/shard_map/all_to_all | solution.py:71
  151.2 12.5 %all-to-all-done.2 = bf16[32,4,24,128]{3,2,1,0:T(8,128)(2,1)S(1)} async-done(((bf16[32,4,24,128]{3,2,1,0:T(8,128)(2,1)}), bf16[32,4,24,128]{3,2,1,0:T(8,128)(2,1)S(1)}, u32[]{:S(2)}, u32[]{:S(2)}) %all-to-all-start.2) | async-done | bytes 786464 | tf_op jit(solution)/shard_map/all_to_all | solution.py:71
  164.0 1.6 fusion.3
  165.7 2.5 %copy.27 = bf16[128,4,1536]{2,1,0:T(4,128)(2,1)} copy(bf16[128,4,1536]{0,2,1:T(8,128)(2,1)S(1)} %pad_maximum_fusion.1) | data formatting | bytes 3145728
  168.2 28.8 %reduce-scatter.2.cloned.1.call-done = bf16[1,24,2048]{2,1,0:T(8,128)(2,1)} async-done(((bf16[16,24,2048]{2,1,0:T(8,128)(2,1)}), bf16[1,24,2048]{2,1,0:T(8,128)(2,1)}) %reduce-scatter.2.cloned.1.call-update) | async-done | bytes 98320 | tf_op jit(solution)/shard_map/reduce_scatter | solution.py:81
  197.0 1.6 multiply_convert_fusion
  (63 shorter events, 14.2 us)
Async XLA Ops:
  7.2 94.1 %all-gather.2.cloned.1.call-start = ((), (), s32[]{:S(2)}) async-start(), calls=%async_computation.4 | async-start | bytes 8912896 | tf_op jit(solution)/shard_map/all_gather | solution.py:28
  11.2 1.1 copy-start.3
  11.2 1.1 copy-start.2
  12.4 10.7 %copy-start.8 = (s32[2,32]{1,0:T(2,128)S(1)}, s32[2,32]{1,0:T(2,128)}, u32[]{:S(2)}) copy-start(s32[2,32]{1,0:T(2,128)} %constant.48.clone) | copy-start | bytes 772
  12.4 10.7 %copy-start.7 = (s32[2,32]{1,0:T(2,128)S(1)}, s32[2,32]{1,0:T(2,128)}, u32[]{:S(2)}) copy-start(s32[2,32]{1,0:T(2,128)} %constant.49.clone) | copy-start | bytes 772
  12.4 23.9 %copy-start.1 = (bf16[1,24,2048]{2,1,0:T(8,128)(2,1)S(1)}, bf16[1,24,2048]{2,1,0:T(8,128)(2,1)}, u32[]{:S(2)}) copy-start(bf16[1,24,2048]{2,1,0:T(8,128)(2,1)} %param.11) | copy-start | bytes 294916
  13.9 22.4 %all-to-all-start = ((bf16[32,4,26,128]{3,1,2,0:T(4,128)(2,1)}), bf16[32,4,26,128]{3,1,2,0:T(4,128)(2,1)S(1)}, u32[]{:S(2)}, u32[]{:S(2)}) async-start(bf16[32,4,26,128]{3,1,2,0:T(4,128)(2,1)} %pad_maximum_fusion.2), calls=%async_computation | async-start | bytes 1703936 | tf_op jit(solution)/shard_map/all_to_all | solution.py:43
  36.3 1.4 copy-start
  37.7 88.3 %all-to-all-start.1 = ((bf16[16,24,2048]{2,1,0:T(8,128)(2,1)}), bf16[16,24,2048]{2,1,0:T(8,128)(2,1)}, u32[]{:S(2)}, u32[]{:S(2)}) async-start(bf16[16,24,2048]{2,1,0:T(8,128)(2,1)} %broadcast_in_dim.138), calls=%async_computation.1 | async-start | bytes 3145728 | tf_op jit(solution)/shard_map/all_to_all | solution.py:22
  51.6 145.4 %reduce-scatter.2.cloned.1.call-start = ((), (), s32[]{:S(2)}) async-start(), calls=%async_computation.5 | async-start | bytes 1671168 | tf_op jit(solution)/shard_map/reduce_scatter | solution.py:81
  101.3 15.2 %collective-permute-start = (bf16[2048,2048]{1,0:T(8,128)(2,1)}, bf16[2048,2048]{1,0:T(8,128)(2,1)S(1)}, u32[]{:S(2)}, u32[]{:S(2)}) collective-permute-start(bf16[2048,2048]{1,0:T(8,128)(2,1)} %all-gather.2.cloned.1.call-done), channel_id=1, source_target_pairs={{0,16},{16,0},{1,17},{17,1},{2,18},{18,2},{3,19},{19,3},{4,20},{20... | collective-permute-start | bytes 25165832 | tf_op jit(solution)/shard_map/ppermute | solution.py:29
  107.2 4.3 %copy-start.4 = (bf16[2048,2048]{1,0:T(8,128)(2,1)S(1)}, bf16[2048,2048]{1,0:T(8,128)(2,1)}, u32[]{:S(2)}) copy-start(bf16[2048,2048]{1,0:T(8,128)(2,1)} %all-gather.2.cloned.1.call-done) | copy-start | bytes 25165828
  116.5 3.2 %copy-start.5 = (bf16[2048,2048]{1,0:T(8,128)(2,1)}, bf16[2048,2048]{1,0:T(8,128)(2,1)S(1)}, u32[]{:S(2)}) copy-start(bf16[2048,2048]{1,0:T(8,128)(2,1)S(1)} %collective-permute-done) | copy-start | bytes 25165828
  126.0 6.5 %copy-start.6 = (bf16[2048,2048]{1,0:T(8,128)(2,1)S(1)}, bf16[2048,2048]{1,0:T(8,128)(2,1)}, u32[]{:S(2)}) copy-start(bf16[2048,2048]{1,0:T(8,128)(2,1)} %copy-done.5) | copy-start | bytes 25165828
  146.0 17.7 %all-to-all-start.2 = ((bf16[32,4,24,128]{3,2,1,0:T(8,128)(2,1)}), bf16[32,4,24,128]{3,2,1,0:T(8,128)(2,1)S(1)}, u32[]{:S(2)}, u32[]{:S(2)}) async-start(bf16[32,4,24,128]{3,2,1,0:T(8,128)(2,1)} %broadcast_select_fusion), calls=%async_computation.2 | async-start | bytes 1572864 | tf_op jit(solution)/shard_map/all_to_all | solution.py:71
Sparse Core Ops, SparseCore 0:
  11.0 90.2 all-gather.1
  126.2 70.7 reduce-scatter.1

commit v6 on v2

--- a/solution.py
+++ b/solution.py
@@ -43,8 +43,9 @@
         hp = hp + jnp.where(ids_t[k][None, None, :] == eidx, (rw_t[k][None, :] * hid_t[k])[None], 0.0)
     hp = hp.reshape(experts * rows, n_all).astype(BF16)
     part = lax.dot_general(hp, og_all, (((1,), (0,)), ((), ())), preferred_element_type=F32)
-    part = part.reshape(experts, rows, width).astype(BF16)
-    part, wcat = lax.optimization_barrier((part, wcat))
+    part = (part / ndp).reshape(experts, rows, width).astype(BF16)
+    down_grad = lax.psum_scatter(part, "expert", scatter_dimension=0, tiled=True)
+    _, wcat = lax.optimization_barrier((part, wcat))
 
     r_t = lax.dot_general(wcat, og_all, (((1,), (1,)), ((), ())), preferred_element_type=F32)
     r_t = r_t.reshape(experts, rows, n_all)
@@ -63,8 +64,6 @@
     up_grad = cot * gate * sig
     pre_grad = jnp.concatenate([gate_grad, up_grad], axis=-1).astype(BF16)
 
-    summed = lax.psum_scatter(part, "expert", scatter_dimension=0, tiled=True)
-    down_grad = (summed.astype(F32) / ndp).astype(BF16)
     return pre_grad, weight_grad, down_grad
 
 

time: 199 us -> 195 us (0.980)
    another operation x1 -> x2, other arithmetic: 1.63 us -> 5.95 us
    eq x4, other arithmetic: 2.66 us -> 0.17 us  [body(): ids_t[k][None, None, :] == eidx]
    reduce_scatter x1, waiting for transfers between devices: 28.6 us -> 26.1 us  [body(): lax.psum_scatter(part, 'expert', scatter_dimension=0, tiled=True)]
    unnamed x25 -> x17, local copies, waits for them, and re-layouts: 5.62 us -> 4.87 us
where the time goes in v6:
time: 195 us; the launch traced here: 194 us
  waiting for transfers between devices  90.7 us (47%)
  matrix products  22.7 us (12%)
  starting transfers between devices  22.3 us (11%)
  blocking collectives  21.5 us (11%)
  between operations  14.3 us (7%)
  other arithmetic  12.3 us (6%)
  local copies, waits for them, and re-layouts  10.5 us (5%)
    all_gather x1, waiting for transfers between devices, body(): og_all = lax.all_gather(out_grad, 'dp', axis=0, tiled=True)  45.2 us
    reduce_scatter x1, waiting for transfers between devices, body(): lax.psum_scatter(part, 'expert', scatter_dimension=0, tiled=True)  26.1 us
    all_to_all x1, blocking collectives, body(): got_h = lax.all_to_all(send_h, 'dp', 0, 0, tiled=True)  21.5 us
    all_to_all x1, starting transfers between devices, body(): lax.all_to_all(jnp.broadcast_to(down_weight, (nex,) + down_weight.shape[1...  14 us
    all_to_all x1, waiting for transfers between devices, body(): got_g = lax.all_to_all(send_g, 'dp', 0, 0, tiled=True)  12.5 us
    dot_general x1, matrix products, body(): lax.dot_general(hp, og_all, (((1,), (0,)), ((), ())), preferred_element_t...  12 us
    dot_general x1, matrix products, body(): lax.dot_general(wcat, og_all, (((1,), (1,)), ((), ())), preferred_element...  10.7 us
    all_to_all x1, starting transfers between devices, body(): got_g = lax.all_to_all(send_g, 'dp', 0, 0, tiled=True)  8.21 us
  transfers between devices with their start and end apart: 4, of which 4 were waited for; matrix products, arithmetic and copies ran while one was open for 23% of the time, Pallas kernels for 0%

profile of v6, /device:TPU:24, one launch (start us, length us, event | category | flops | bytes accessed | tf_op | source)
XLA Modules:
  0.0 194.4 jit_solution(4540025526134113326)
XLA Ops:
  7.2 0.7 all-gather.2.cloned.1.call-update
  7.9 1.9 fusion.11
  9.8 0.7 copy.28
  10.5 0.7 copy.29
  11.2 0.5 fusion
  11.9 0.7 copy.19
  12.6 21.5 %all_to_all.15 = bf16[32,4,26,128]{3,1,2,0:T(4,128)(2,1)S(1)} all-to-all(bf16[32,4,26,128]{3,1,2,0:T(4,128)(2,1)S(1)} %copy.19), channel_id=1, replica_groups=mesh['dp'=32,'expert'=16] {'dp'}, dimensions={0} | all-to-all | bytes 1703936 | tf_op jit(solution)/shard_map/all_to_all | solution.py:34
  34.1 1.3 broadcast_in_dim.115
  35.5 14.0 %all-to-all-start.1 = ((bf16[16,24,2048]{2,1,0:T(8,128)(2,1)}), bf16[16,24,2048]{2,1,0:T(8,128)(2,1)}, u32[]{:S(2)}, u32[]{:S(2)}) async-start(bf16[16,24,2048]{2,1,0:T(8,128)(2,1)} %broadcast_in_dim.115), calls=%async_computation.1 | async-start | bytes 3145728 | tf_op jit(solution)/shard_map/all_to_all | solution.py:19
  49.5 0.4 copy_bitcast_fusion
  50.3 1.8 slice_multiply_fusion.3
  52.1 0.2 copy.43
  53.2 4.3 %add_convert_fusion = bf16[16,24,4096]{2,1,0:T(8,128)(2,1)} fusion(f32[24,4096]{1,0:T(8,128)S(1)} %bitcast.82, f32[24,4096]{1,0:T(8,128)S(1)} %bitcast.83, f32[24,4096]{1,0:T(8,128)S(1)} %bitcast.84, f32[24,4096]{1,0:T(8,128)S(1)} %bitcast.85, pred[16,4096]{1,0:T(8,128)(4,1)S(1)} %iota_compare_fusion, pred[16,4096]{1,0:T(8,128)(4,1)S(1)} %iota_compare_fusion.1, ...), kind=kLoop, calls=%fused_computation.4 | loop fusion | flops 12582912 | bytes 4980736 | tf_op jit(solution)/shard_map/convert.12
  57.5 45.2 %all-gather.2.cloned.1.call-done = bf16[4096,2048]{1,0:T(8,128)(2,1)} async-done(((bf16[128,2048]{1,0:T(8,128)(2,1)}), bf16[4096,2048]{1,0:T(8,128)(2,1)}) %all-gather.2.cloned.1.call-update) | async-done | bytes 16777232 | tf_op jit(solution)/shard_map/all_gather | solution.py:24
  102.8 12.0 %multiply_convert_fusion = bf16[384,2048]{1,0:T(8,128)(2,1)} fusion(bf16[384,4096]{1,0:T(8,128)(2,1)} %bitcast.80, bf16[4096,2048]{1,0:T(8,128)(2,1)} %all-gather.2.cloned.1.call-done), kind=kOutput, calls=%fused_computation.5 | convolution fusion | flops 6444023808 | bytes 21495808 | tf_op jit(solution)/shard_map/dot_general | solution.py:45
  114.8 6.1 %all-to-all-done.1 = bf16[16,24,2048]{2,1,0:T(8,128)(2,1)} async-done(((bf16[16,24,2048]{2,1,0:T(8,128)(2,1)}), bf16[16,24,2048]{2,1,0:T(8,128)(2,1)}, u32[]{:S(2)}, u32[]{:S(2)}) %all-to-all-start.1) | async-done | bytes 1572896 | tf_op jit(solution)/shard_map/all_to_all | solution.py:19
  121.0 10.7 %fusion.14 = f32[384,4096]{1,0:T(8,128)S(1)} fusion(bf16[384,2048]{1,0:T(8,128)(2,1)} %bitcast.18, bf16[4096,2048]{1,0:T(8,128)(2,1)} %all-gather.2.cloned.1.call-done), kind=kOutput, calls=%fused_computation.53 | convolution fusion | flops 6442450944 | bytes 24641536 | tf_op jit(solution)/shard_map/dot_general | solution.py:50
  131.7 3.4 %select_reduce_fusion.3 = (bf16[24,4096]{1,0:T(8,128)(2,1)S(1)}, bf16[24,4096]{1,0:T(8,128)(2,1)S(1)}, bf16[24,4096]{1,0:T(8,128)(2,1)S(1)}, bf16[24,4096]{1,0:T(8,128)(2,1)S(1)}) fusion(f32[16,24,4096]{2,1,0:T(8,128)S(1)} %bitcast.79, pred[16,4096]{1,0:T(8,128)(4,1)S(1)} %iota_compare_fusion.3, pred[16,4096]{1,0:T(8,128)(4,1)S(1)} %iota_compare_fusion, ...), kind=kLoop, calls=%fused_computation.3 | loop fusion | flops 12189696 | bytes 7340032 | tf_op jit(solution)/shard_map/reduce_sum | solution.py:53
  135.3 1.2 copy.21
  136.5 8.2 %all-to-all-start.2 = ((bf16[32,4,24,128]{3,2,1,0:T(8,128)(2,1)}), bf16[32,4,24,128]{3,2,1,0:T(8,128)(2,1)S(1)}, u32[]{:S(2)}, u32[]{:S(2)}) async-start(bf16[32,4,24,128]{3,2,1,0:T(8,128)(2,1)} %copy.21), calls=%async_computation.2 | async-start | bytes 1572864 | tf_op jit(solution)/shard_map/all_to_all | solution.py:57
  144.7 12.5 %all-to-all-done.2 = bf16[32,4,24,128]{3,2,1,0:T(8,128)(2,1)S(1)} async-done(((bf16[32,4,24,128]{3,2,1,0:T(8,128)(2,1)}), bf16[32,4,24,128]{3,2,1,0:T(8,128)(2,1)S(1)}, u32[]{:S(2)}, u32[]{:S(2)}) %all-to-all-start.2) | async-done | bytes 786464 | tf_op jit(solution)/shard_map/all_to_all | solution.py:57
  157.2 1.6 fusion.3
  158.9 2.5 %copy.23 = bf16[128,4,1536]{2,1,0:T(4,128)(2,1)} copy(bf16[128,4,1536]{0,2,1:T(8,128)(2,1)S(1)} %pad_maximum_fusion) | data formatting | bytes 3145728
  161.4 26.1 %reduce-scatter.2.cloned.1.call-done = bf16[1,24,2048]{2,1,0:T(8,128)(2,1)} async-done(((bf16[16,24,2048]{2,1,0:T(8,128)(2,1)}), bf16[1,24,2048]{2,1,0:T(8,128)(2,1)}) %reduce-scatter.2.cloned.1.call-update) | async-done | bytes 98320 | tf_op jit(solution)/shard_map/reduce_scatter | solution.py:47
  (31 shorter events, 1.8 us)
Async XLA Ops:
  7.2 95.6 %all-gather.2.cloned.1.call-start = ((), (), s32[]{:S(2)}) async-start(), calls=%async_computation.4 | async-start | bytes 17301504 | tf_op jit(solution)/shard_map/all_gather | solution.py:24
  9.8 1.4 copy-start.2
  9.8 1.4 copy-start.1
  11.9 22.2 %copy-start = (bf16[1,24,2048]{2,1,0:T(8,128)(2,1)S(1)}, bf16[1,24,2048]{2,1,0:T(8,128)(2,1)}, u32[]{:S(2)}) copy-start(bf16[1,24,2048]{2,1,0:T(8,128)(2,1)} %param.9) | copy-start | bytes 294916
  35.5 85.5 %all-to-all-start.1 = ((bf16[16,24,2048]{2,1,0:T(8,128)(2,1)}), bf16[16,24,2048]{2,1,0:T(8,128)(2,1)}, u32[]{:S(2)}, u32[]{:S(2)}) async-start(bf16[16,24,2048]{2,1,0:T(8,128)(2,1)} %broadcast_in_dim.115), calls=%async_computation.1 | async-start | bytes 3145728 | tf_op jit(solution)/shard_map/all_to_all | solution.py:19
  49.5 138.1 %reduce-scatter.2.cloned.1.call-start = ((), (), s32[]{:S(2)}) async-start(), calls=%async_computation.5 | async-start | bytes 1671168 | tf_op jit(solution)/shard_map/reduce_scatter | solution.py:47
  136.5 20.7 %all-to-all-start.2 = ((bf16[32,4,24,128]{3,2,1,0:T(8,128)(2,1)}), bf16[32,4,24,128]{3,2,1,0:T(8,128)(2,1)S(1)}, u32[]{:S(2)}, u32[]{:S(2)}) async-start(bf16[32,4,24,128]{3,2,1,0:T(8,128)(2,1)} %copy.21), calls=%async_computation.2 | async-start | bytes 1572864 | tf_op jit(solution)/shard_map/all_to_all | solution.py:57
Sparse Core Ops, SparseCore 0:
  11.1 91.6 all-gather.1
  114.9 72.5 reduce-scatter.1

commit v7 on v6

--- a/solution.py
+++ b/solution.py
@@ -44,8 +44,9 @@
     hp = hp.reshape(experts * rows, n_all).astype(BF16)
     part = lax.dot_general(hp, og_all, (((1,), (0,)), ((), ())), preferred_element_type=F32)
     part = (part / ndp).reshape(experts, rows, width).astype(BF16)
-    down_grad = lax.psum_scatter(part, "expert", scatter_dimension=0, tiled=True)
-    _, wcat = lax.optimization_barrier((part, wcat))
+    dense = part.reshape(experts, 2 * rows, width // 2)
+    dense, og_all = lax.optimization_barrier((dense, og_all))
+    down_grad = lax.psum_scatter(dense, "expert", scatter_dimension=0, tiled=True).reshape(1, rows, width)
 
     r_t = lax.dot_general(wcat, og_all, (((1,), (1,)), ((), ())), preferred_element_type=F32)
     r_t = r_t.reshape(experts, rows, n_all)

time: 195 us -> 200 us (1.026)
  local copies, waits for them, and re-layouts: 10.5 us -> 15.7 us
    reduce_scatter x1, waiting for transfers between devices: 26.1 us -> 29.8 us  [body(): lax.psum_scatter(dense, 'expert', scatter_dimension=0, tiled=True)]
    all_to_all x1, waiting for transfers between devices: 6.13 us -> 2.54 us  [body(): lax.all_to_all(jnp.broadcast_to(down_weight, (nex,) + down_weight.shape[1...]
    convert_element_type x0 -> x1, local copies, waits for them, and re-layouts: none -> 3.6 us  [body(): part = (part / ndp).reshape(experts, rows, width).astype(BF16)]
  transfers between devices with their start and end apart: 4 -> 4, of which waited for: 4 -> 4; matrix products, arithmetic and copies ran while one was open for 23% -> 25% of each run, Pallas kernels for 0% -> 0%
where the time goes in v7:
time: 200 us
  waiting for transfers between devices  90.8 us (45%)
  matrix products  22.7 us (11%)
  starting transfers between devices  22.3 us (11%)
  blocking collectives  21.5 us (11%)
  local copies, waits for them, and re-layouts  15.7 us (8%)
  between operations  14.3 us (7%)
  other arithmetic  12.3 us (6%)
    all_gather x1, waiting for transfers between devices, body(): og_all = lax.all_gather(out_grad, 'dp', axis=0, tiled=True)  45.2 us
    reduce_scatter x1, waiting for transfers between devices, body(): lax.psum_scatter(dense, 'expert', scatter_dimension=0, tiled=True)  29.8 us
    all_to_all x1, blocking collectives, body(): got_h = lax.all_to_all(send_h, 'dp', 0, 0, tiled=True)  21.5 us
    all_to_all x1, starting transfers between devices, body(): lax.all_to_all(jnp.broadcast_to(down_weight, (nex,) + down_weight.shape[1...  14 us
    all_to_all x1, waiting for transfers between devices, body(): got_g = lax.all_to_all(send_g, 'dp', 0, 0, tiled=True)  12.5 us
    dot_general x1, matrix products, body(): lax.dot_general(hp, og_all, (((1,), (0,)), ((), ())), preferred_element_t...  12 us
    dot_general x1, matrix products, body(): lax.dot_general(wcat, og_all, (((1,), (1,)), ((), ())), preferred_element...  10.7 us
    all_to_all x1, starting transfers between devices, body(): got_g = lax.all_to_all(send_g, 'dp', 0, 0, tiled=True)  8.21 us
  transfers between devices with their start and end apart: 4, of which 4 were waited for; matrix products, arithmetic and copies ran while one was open for 25% of the time, Pallas kernels for 0%

profile of v7, /device:TPU:24, one launch (start us, length us, event | category | flops | bytes accessed | tf_op | source)
XLA Modules:
  0.0 199.6 jit_solution(12277648479053517612)
XLA Ops:
  7.2 0.7 all-gather.2.cloned.1.call-update
  7.9 1.9 fusion.11
  9.8 0.7 copy.28
  10.5 0.7 copy.29
  11.3 0.5 fusion
  11.9 0.7 copy.19
  12.6 21.5 %all_to_all.15 = bf16[32,4,26,128]{3,1,2,0:T(4,128)(2,1)S(1)} all-to-all(bf16[32,4,26,128]{3,1,2,0:T(4,128)(2,1)S(1)} %copy.19), channel_id=1, replica_groups=mesh['dp'=32,'expert'=16] {'dp'}, dimensions={0} | all-to-all | bytes 1703936 | tf_op jit(solution)/shard_map/all_to_all | solution.py:34
  34.1 1.3 broadcast_in_dim.115
  35.5 14.0 %all-to-all-start.1 = ((bf16[16,24,2048]{2,1,0:T(8,128)(2,1)}), bf16[16,24,2048]{2,1,0:T(8,128)(2,1)}, u32[]{:S(2)}, u32[]{:S(2)}) async-start(bf16[16,24,2048]{2,1,0:T(8,128)(2,1)} %broadcast_in_dim.115), calls=%async_computation.1 | async-start | bytes 3145728 | tf_op jit(solution)/shard_map/all_to_all | solution.py:19
  50.3 1.8 slice_multiply_fusion.3
  53.2 4.3 %add_convert_fusion = bf16[16,24,4096]{2,1,0:T(8,128)(2,1)} fusion(f32[24,4096]{1,0:T(8,128)S(1)} %bitcast.82, f32[24,4096]{1,0:T(8,128)S(1)} %bitcast.83, f32[24,4096]{1,0:T(8,128)S(1)} %bitcast.84, f32[24,4096]{1,0:T(8,128)S(1)} %bitcast.85, pred[16,4096]{1,0:T(8,128)(4,1)S(1)} %iota_compare_fusion, pred[16,4096]{1,0:T(8,128)(4,1)S(1)} %iota_compare_fusion.1, ...), kind=kLoop, calls=%fused_computation.4 | loop fusion | flops 12582912 | bytes 4980736 | tf_op jit(solution)/shard_map/convert.12
  57.5 45.2 %all-gather.2.cloned.1.call-done = bf16[4096,2048]{1,0:T(8,128)(2,1)} async-done(((bf16[128,2048]{1,0:T(8,128)(2,1)}), bf16[4096,2048]{1,0:T(8,128)(2,1)}) %all-gather.2.cloned.1.call-update) | async-done | bytes 16777232 | tf_op jit(solution)/shard_map/all_gather | solution.py:24
  102.8 12.0 %multiply_convert_fusion = bf16[384,2048]{1,0:T(8,128)(2,1)} fusion(bf16[384,4096]{1,0:T(8,128)(2,1)} %bitcast.81, bf16[4096,2048]{1,0:T(8,128)(2,1)} %all-gather.2.cloned.1.call-done), kind=kOutput, calls=%fused_computation.5 | convolution fusion | flops 6444023808 | bytes 21495808 | tf_op jit(solution)/shard_map/dot_general | solution.py:45
  114.8 3.6 %convert_element_type.65 = bf16[16,48,1024]{2,1,0:T(8,128)(2,1)} reshape(bf16[384,2048]{1,0:T(8,128)(2,1)} %multiply_convert_fusion) | data formatting | bytes 3145728 | tf_op jit(solution)/shard_map/convert_element_type | solution.py:46
  118.4 2.5 %all-to-all-done.1 = bf16[16,24,2048]{2,1,0:T(8,128)(2,1)} async-done(((bf16[16,24,2048]{2,1,0:T(8,128)(2,1)}), bf16[16,24,2048]{2,1,0:T(8,128)(2,1)}, u32[]{:S(2)}, u32[]{:S(2)}) %all-to-all-start.1) | async-done | bytes 1572896 | tf_op jit(solution)/shard_map/all_to_all | solution.py:19
  121.0 10.7 %fusion.14 = f32[4096,384]{0,1:T(8,128)S(1)} fusion(bf16[4096,2048]{1,0:T(8,128)(2,1)} %all-gather.2.cloned.1.call-done, bf16[384,2048]{1,0:T(8,128)(2,1)} %bitcast.17), kind=kOutput, calls=%fused_computation.53 | convolution fusion | flops 6442450944 | bytes 24641536 | tf_op jit(solution)/shard_map/dot_general | solution.py:51
  131.7 3.4 %select_reduce_fusion.3 = (bf16[24,4096]{1,0:T(8,128)(2,1)S(1)}, bf16[24,4096]{1,0:T(8,128)(2,1)S(1)}, bf16[24,4096]{1,0:T(8,128)(2,1)S(1)}, bf16[24,4096]{1,0:T(8,128)(2,1)S(1)}) fusion(f32[16,24,4096]{2,1,0:T(8,128)S(1)} %bitcast.80, pred[16,4096]{1,0:T(8,128)(4,1)S(1)} %iota_compare_fusion.3, pred[16,4096]{1,0:T(8,128)(4,1)S(1)} %iota_compare_fusion, ...), kind=kLoop, calls=%fused_computation.3 | loop fusion | flops 12189696 | bytes 7340032 | tf_op jit(solution)/shard_map/reduce_sum | solution.py:54
  135.3 1.2 copy.21
  136.5 8.2 %all-to-all-start.2 = ((bf16[32,4,24,128]{3,2,1,0:T(8,128)(2,1)}), bf16[32,4,24,128]{3,2,1,0:T(8,128)(2,1)S(1)}, u32[]{:S(2)}, u32[]{:S(2)}) async-start(bf16[32,4,24,128]{3,2,1,0:T(8,128)(2,1)} %copy.21), calls=%async_computation.2 | async-start | bytes 1572864 | tf_op jit(solution)/shard_map/all_to_all | solution.py:58
  144.7 12.5 %all-to-all-done.2 = bf16[32,4,24,128]{3,2,1,0:T(8,128)(2,1)S(1)} async-done(((bf16[32,4,24,128]{3,2,1,0:T(8,128)(2,1)}), bf16[32,4,24,128]{3,2,1,0:T(8,128)(2,1)S(1)}, u32[]{:S(2)}, u32[]{:S(2)}) %all-to-all-start.2) | async-done | bytes 786464 | tf_op jit(solution)/shard_map/all_to_all | solution.py:58
  157.2 1.6 fusion.3
  158.9 2.5 %copy.23 = bf16[128,4,1536]{2,1,0:T(4,128)(2,1)} copy(bf16[128,4,1536]{0,2,1:T(8,128)(2,1)S(1)} %pad_maximum_fusion) | data formatting | bytes 3145728
  161.4 29.8 %reduce-scatter.2.cloned.1.call-done = bf16[1,48,1024]{2,1,0:T(8,128)(2,1)} async-done(((bf16[16,48,1024]{2,1,0:T(8,128)(2,1)}), bf16[1,48,1024]{2,1,0:T(8,128)(2,1)}) %reduce-scatter.2.cloned.1.call-update) | async-done | bytes 98320 | tf_op jit(solution)/shard_map/reduce_scatter | solution.py:49
  191.2 1.6 reshape.200
  (33 shorter events, 2.4 us)
Async XLA Ops:
  7.2 95.6 %all-gather.2.cloned.1.call-start = ((), (), s32[]{:S(2)}) async-start(), calls=%async_computation.4 | async-start | bytes 17301504 | tf_op jit(solution)/shard_map/all_gather | solution.py:24
  9.8 1.4 copy-start.2
  9.8 1.4 copy-start.1
  11.9 22.2 %copy-start = (bf16[1,24,2048]{2,1,0:T(8,128)(2,1)S(1)}, bf16[1,24,2048]{2,1,0:T(8,128)(2,1)}, u32[]{:S(2)}) copy-start(bf16[1,24,2048]{2,1,0:T(8,128)(2,1)} %param.9) | copy-start | bytes 294916
  35.5 85.5 %all-to-all-start.1 = ((bf16[16,24,2048]{2,1,0:T(8,128)(2,1)}), bf16[16,24,2048]{2,1,0:T(8,128)(2,1)}, u32[]{:S(2)}, u32[]{:S(2)}) async-start(bf16[16,24,2048]{2,1,0:T(8,128)(2,1)} %broadcast_in_dim.115), calls=%async_computation.1 | async-start | bytes 3145728 | tf_op jit(solution)/shard_map/all_to_all | solution.py:19
  49.5 141.7 %reduce-scatter.2.cloned.1.call-start = ((), (), s32[]{:S(2)}) async-start(), calls=%async_computation.5 | async-start | bytes 1671168 | tf_op jit(solution)/shard_map/reduce_scatter | solution.py:49
  136.5 20.7 %all-to-all-start.2 = ((bf16[32,4,24,128]{3,2,1,0:T(8,128)(2,1)}), bf16[32,4,24,128]{3,2,1,0:T(8,128)(2,1)S(1)}, u32[]{:S(2)}, u32[]{:S(2)}) async-start(bf16[32,4,24,128]{3,2,1,0:T(8,128)(2,1)} %copy.21), calls=%async_computation.2 | async-start | bytes 1572864 | tf_op jit(solution)/shard_map/all_to_all | solution.py:58
Sparse Core Ops, SparseCore 0:
  11.1 91.6 all-gather.1
  118.5 72.6 reduce-scatter.1
